TPU v7x, 128 devices: a whole 4x4x4 slice. The times are simulated.
128 devices in a mesh: seq: 16 (over x, y), resp: 8 (over z, core).
Axes of the slice: x: 4, y: 4, z: 4, core: 2. Of those that a mesh axis runs over, the one named last changes fastest.
Arguments:
- prompt_keys: bfloat16 [2, 2048, 1024], P(None, 'seq'), may hold values from -6.1 to 6.1
- prompt_values: bfloat16 [2, 2048, 1024], P(None, 'seq'), may hold values from -6 to 6
- resp_query: bfloat16 [16, 1024, 8192], P('resp', None, 'seq'), may hold values from -121 to 121
- resp_keys: bfloat16 [16, 1024, 1024], P('resp'), may hold values from -6 to 6
- resp_values: bfloat16 [16, 1024, 1024], P('resp'), may hold values from -6 to 6
- prompt_x: bfloat16 [2, 2048, 16384], P(None, 'seq', 'resp'), may hold values from -6 to 6
- prompt_dt: float32 [2, 256, 2048], P(None, 'resp', 'seq'), may hold values from 0 to 0.5, as said below
- prompt_b: bfloat16 [2, 2048, 128], P(None, 'seq'), may hold values from -6 to 6
- prompt_c: bfloat16 [2, 2048, 128], P(None, 'seq'), may hold values from -0.5 to 0.5
- resp_x: bfloat16 [16, 1024, 16384], P('resp', None, 'seq'), may hold values from -6 to 6
- resp_dt: float32 [16, 256, 1024], P('resp', 'seq'), may hold values from 0 to 0.5, as said below
- resp_b: bfloat16 [16, 1024, 128], P('resp'), may hold values from -6 to 6
- resp_c: bfloat16 [16, 1024, 128], P('resp'), may hold values from -0.5 to 0.5
- ssm_rate: float32 [256], replicated, may hold values from 0.7 to 1.4
- resp_group: int32 [16], P('resp'), may hold values from 0 to 1
- resp_len: int32 [16], P('resp'), may hold values from 1 to 1024, 10240 in all
Outputs:
- resp_attn_out: bfloat16 [16, 1024, 8192], P('resp', None, 'seq')
- resp_ssm_out: bfloat16 [16, 1024, 16384], P('resp', None, 'seq')
- prompt_ssm_out: bfloat16 [2, 2048, 16384], P(None, 'seq', 'resp')
Inputs may be any that keep to these rules, and one draw needn't show every extreme that they name: `prompt_dt`: positive step sizes. `resp_dt`: positive step sizes.
All inputs are finite; a program needn't handle non-finite values. No bound on the sum of `resp_len` on one device may be relied on, other than what follows from the above.
Results may differ from a plain program's by a relative error of at most 0.0048.
Values may be sent and summed in bfloat16 or wider, within the bound.
No kernel may reach another device: no remote copies, remote signals or barrier semaphores. Data moves between devices by JAX's collectives and lax.ppermute only.
A program may use at most 192 MiB of HBM per device.

v0:
```python
import math

import jax
import jax.numpy as jnp
from jax import lax
from jax.experimental import pallas as pl
from jax.experimental.pallas import tpu as pltpu
from jax.sharding import PartitionSpec as P

HDIM = 128
SP = 64
NST = 128
QS = 128


EPS = 1e-05


def from_behind(block, axis, distance):
    devices = range(lax.axis_size(axis))
    route = [(i - distance, i) for i in devices if i - distance in devices]
    return lax.ppermute(block, axis, route)


def broadcast(value, axis, source):
    kept = jnp.where(lax.axis_index(axis) == source, value, 0).astype(value.dtype)
    return lax.psum(kept, axis)


def block_pass(inputs, steps, b_rows, c_rows, rates, state):
    exponent = jnp.cumsum(-steps * rates[:, None], axis=1)
    width = inputs.shape[0]
    lower = lax.broadcasted_iota(jnp.int32, (width, width), 0) >= lax.broadcasted_iota(
        jnp.int32, (width, width), 1
    )
    spread = jnp.where(lower[None], exponent[:, :, None] - exponent[:, None, :], -jnp.inf)
    gram = jnp.dot(c_rows, b_rows.T, preferred_element_type=jnp.float32)
    mixing = (jnp.exp(spread) * gram[None] * steps[:, None, :]).astype(jnp.bfloat16)
    local = jnp.einsum("hts,shp->thp", mixing, inputs, preferred_element_type=jnp.float32)
    carried = jnp.einsum(
        "tn,hpn->thp", c_rows.astype(jnp.float32), state, precision=lax.Precision.HIGHEST
    )
    output = local + carried * jnp.exp(exponent).T[:, :, None]
    last = exponent[:, -1]
    weighted = (
        inputs.astype(jnp.float32) * (jnp.exp(last[:, None] - exponent) * steps).T[:, :, None]
    ).astype(jnp.bfloat16)
    fresh = jnp.einsum("thp,tn->hpn", weighted, b_rows, preferred_element_type=jnp.float32)
    return (output, jnp.exp(last)[:, None, None] * state + fresh, exponent)


def sequence_pass(inputs, steps, b_rows, c_rows, rates):
    window_extent = inputs.shape[0]
    heads = steps.shape[0]
    blocks = window_extent // QS
    xs = inputs.reshape(blocks, QS, heads, SP)
    ss = steps.reshape(heads, blocks, QS).transpose(1, 0, 2)
    bs = b_rows.reshape(blocks, QS, NST)
    cs = c_rows.reshape(blocks, QS, NST)

    def advance(carry, block):
        state, offset = carry
        out, state_next, exponent = block_pass(block[0], block[1], block[2], block[3], rates, state)
        return ((state_next, offset + exponent[:, -1]), (out, offset[:, None] + exponent))

    start = (jnp.zeros((heads, SP, NST), jnp.float32), jnp.zeros((heads,), jnp.float32))
    (final, total), (outs, decays_to) = lax.scan(advance, start, (xs, ss, bs, cs))
    decays_to = decays_to.transpose(1, 0, 2).reshape(heads, window_extent)
    return (outs.reshape(window_extent, heads, SP), final, decays_to, total)


def chunked_pass(inputs, steps, b_rows, c_rows, rates):
    window_extent = inputs.shape[0]
    heads = steps.shape[0]
    blocks = window_extent // QS
    xs = inputs.reshape(blocks, QS, heads, SP).transpose(0, 2, 1, 3)
    ss = steps.reshape(heads, blocks, QS).transpose(1, 0, 2)
    bs = b_rows.reshape(blocks, QS, NST)
    cs = c_rows.reshape(blocks, QS, NST)
    exponent = jnp.cumsum(-ss * rates[None, :, None], axis=2)
    lower = lax.broadcasted_iota(jnp.int32, (QS, QS), 0) >= lax.broadcasted_iota(
        jnp.int32, (QS, QS), 1
    )
    spread = jnp.where(
        lower[None, None], exponent[:, :, :, None] - exponent[:, :, None, :], -jnp.inf
    )
    gram = jnp.einsum("ctn,cun->ctu", cs, bs, preferred_element_type=jnp.float32)
    mixing = (jnp.exp(spread) * gram[:, None] * ss[:, :, None, :]).astype(jnp.bfloat16)
    local = jnp.einsum("chtu,chup->chtp", mixing, xs, preferred_element_type=jnp.float32)
    last = exponent[:, :, -1]
    weighted = (
        xs.astype(jnp.float32) * (jnp.exp(last[:, :, None] - exponent) * ss)[:, :, :, None]
    ).astype(jnp.bfloat16)
    fresh = jnp.einsum("chup,cun->chpn", weighted, bs, preferred_element_type=jnp.float32)
    decay = jnp.exp(last)
    state = jnp.zeros((heads, SP, NST), jnp.float32)
    offset = jnp.zeros((heads,), jnp.float32)
    befores = []
    offsets = []
    for index in range(blocks):
        befores.append(state)
        offsets.append(offset)
        state = decay[index][:, None, None] * state + fresh[index]
        offset = offset + last[index]
    before = jnp.stack(befores)
    carried = jnp.einsum(
        "ctn,chpn->chtp", cs.astype(jnp.float32), before, precision=lax.Precision.HIGHEST
    )
    output = local + carried * jnp.exp(exponent)[:, :, :, None]
    decays_to = jnp.stack(offsets)[:, :, None] + exponent
    output = output.transpose(0, 2, 1, 3).reshape(window_extent, heads, SP)
    decays_to = decays_to.transpose(1, 0, 2).reshape(heads, window_extent)
    return (output, state, decays_to, offset)


def head_norm(values):
    scale = lax.rsqrt(jnp.mean(values * values, axis=-1, keepdims=True) + EPS)
    return (values * scale).reshape(values.shape[0], -1)


def linkage_merge(earlier, later):
    return (earlier[0] * later[0], later[0][:, :, None, None] * earlier[1] + later[1])


def body(
    prompt_keys,
    prompt_values,
    resp_query,
    resp_keys,
    resp_values,
    prompt_x,
    prompt_dt,
    prompt_b,
    prompt_c,
    resp_x,
    resp_dt,
    resp_b,
    resp_c,
    ssm_rate,
    resp_group,
    resp_len,
):
    seq_index = lax.axis_index("seq")
    resp_index = lax.axis_index("resp")
    seq_count = lax.axis_size("seq")
    prompt_count = prompt_x.shape[0]
    prompt_heads = prompt_dt.shape[1]
    resp_heads = resp_dt.shape[1]
    responses_here = resp_x.shape[0]
    slots = resp_x.shape[1]
    memory_head_number = prompt_keys.shape[2] // HDIM
    repeat = seq_count // memory_head_number
    shard_rows = prompt_keys.shape[1]
    spread_keys = jnp.repeat(
        prompt_keys.reshape(prompt_count, shard_rows, memory_head_number, HDIM), repeat, axis=2
    ).reshape(prompt_count, shard_rows, seq_count * HDIM)
    spread_values = jnp.repeat(
        prompt_values.reshape(prompt_count, shard_rows, memory_head_number, HDIM), repeat, axis=2
    ).reshape(prompt_count, shard_rows, seq_count * HDIM)
    moved_keys, moved_values = (
        lax.all_to_all(spread_keys, "seq", split_axis=2, concat_axis=1, tiled=True),
        lax.all_to_all(spread_values, "seq", split_axis=2, concat_axis=1, tiled=True),
    )
    resp_rates = lax.dynamic_slice_in_dim(ssm_rate, seq_index * resp_heads, resp_heads)
    resp_locals = []
    for item in range(responses_here):
        resp_locals.append(
            chunked_pass(resp_x[item], resp_dt[item], resp_b[item], resp_c[item], resp_rates)
        )
    prompt_rates = lax.dynamic_slice_in_dim(ssm_rate, resp_index * prompt_heads, prompt_heads)
    local_outs = []
    local_states = []
    prompt_decays = []
    log_totals = []
    for prompt in range(prompt_count):
        out, final, decays_to, total = sequence_pass(
            prompt_x[prompt], prompt_dt[prompt], prompt_b[prompt], prompt_c[prompt], prompt_rates
        )
        local_outs.append(out)
        local_states.append(final)
        prompt_decays.append(decays_to)
        log_totals.append(total)
    local_state = jnp.stack(local_states)
    decay_total = jnp.exp(jnp.stack(log_totals))
    gathered_states = lax.all_gather(local_state, "seq")
    gathered_decays = lax.all_gather(decay_total, "seq")
    shard = lax.broadcasted_iota(jnp.int32, (seq_count, seq_count), 0)
    later = lax.broadcasted_iota(jnp.int32, (seq_count, seq_count), 1)
    between = (later > shard) & (later < seq_index)
    after = later > shard
    factors = gathered_decays[None]
    before_weights = jnp.prod(jnp.where(between[:, :, None, None], factors, 1.0), axis=1)
    before_weights = jnp.where((shard[:, 0] < seq_index)[:, None, None], before_weights, 0.0)
    final_weights = jnp.prod(jnp.where(after[:, :, None, None], factors, 1.0), axis=1)
    arriving_state = jnp.sum(before_weights[:, :, :, None, None] * gathered_states, axis=0)
    inclusive = jnp.sum(final_weights[:, :, :, None, None] * gathered_states, axis=0)
    prompt_outs = []
    for prompt in range(prompt_count):
        carried = jnp.einsum(
            "tn,hdn->thd",
            prompt_c[prompt].astype(jnp.float32),
            arriving_state[prompt],
            precision=lax.Precision.HIGHEST,
        )
        corrected = local_outs[prompt] + jnp.exp(prompt_decays[prompt]).T[:, :, None] * carried
        prompt_outs.append(head_norm(corrected).astype(jnp.bfloat16))
    prompt_ssm_out = jnp.stack(prompt_outs)
    finals = inclusive
    ratio = seq_count // lax.axis_size("resp")
    piece = lax.dynamic_slice_in_dim(finals, seq_index % ratio * resp_heads, resp_heads, 1)
    piece, resp_query = lax.optimization_barrier((piece, resp_query))
    start_states = broadcast(piece, "resp", seq_index // ratio)
    positions = lax.broadcasted_iota(jnp.int32, (slots,), 0)
    resp_outs = []
    for item in range(responses_here):
        out, final, decays_to, total = resp_locals[item]
        initial = lax.dynamic_index_in_dim(start_states, resp_group[item], 0, keepdims=False)
        carried = jnp.einsum(
            "tn,hdn->thd",
            resp_c[item].astype(jnp.float32),
            initial,
            precision=lax.Precision.HIGHEST,
        )
        corrected = out + jnp.exp(decays_to).T[:, :, None] * carried
        valid = positions < resp_len[item]
        resp_outs.append(jnp.where(valid[:, None], head_norm(corrected), 0.0).astype(jnp.bfloat16))
    resp_ssm_out = jnp.stack(resp_outs)
    heads_here = resp_query.shape[2] // HDIM
    own_head = seq_index // repeat
    resp_attn_out = response_attention(
        resp_query, moved_keys, moved_values, resp_keys, resp_values, resp_group, resp_len, own_head
    )
    return (resp_attn_out, resp_ssm_out, prompt_ssm_out)


ROWS = 512

def response_attention(resp_query, prompt_keys, prompt_values, resp_keys, resp_values, group, length, head):
    items, slots, width = resp_query.shape
    heads = width // HDIM
    rows = slots * heads
    queries = resp_query.reshape(items, rows, HDIM)
    prompt_len = prompt_keys.shape[1]
    tile = min(ROWS, rows)
    scale = 1.0 / math.sqrt(HDIM)

    def kernel(group_ref, len_ref, head_ref, q_ref, pk_ref, pv_ref, rk_ref, rv_ref, o_ref):
        item = pl.program_id(0)
        block = pl.program_id(1)
        window_extent = len_ref[item]
        first = block * (tile // heads)

        @pl.when(first >= window_extent)
        def _():
            o_ref[...] = jnp.zeros_like(o_ref)

        @pl.when(first < window_extent)
        def _():
            q = q_ref[0]
            dims = (((1,), (1,)), ((), ()))
            s1 = lax.dot_general(q, pk_ref[0], dims, preferred_element_type=jnp.float32) * scale
            s2 = lax.dot_general(q, rk_ref[0], dims, preferred_element_type=jnp.float32) * scale
            position = first + lax.broadcasted_iota(jnp.int32, (tile, 1), 0) // heads
            column = lax.broadcasted_iota(jnp.int32, s2.shape, 1)
            s2 = jnp.where(column <= position, s2, -jnp.inf)
            top = jnp.maximum(
                jnp.max(s1, axis=1, keepdims=True), jnp.max(s2, axis=1, keepdims=True)
            )
            e1 = jnp.exp(s1 - top)
            e2 = jnp.exp(s2 - top)
            total = jnp.sum(e1, axis=1, keepdims=True) + jnp.sum(e2, axis=1, keepdims=True)
            mixed = jnp.dot(
                e1.astype(jnp.bfloat16), pv_ref[0], preferred_element_type=jnp.float32
            ) + jnp.dot(e2.astype(jnp.bfloat16), rv_ref[0], preferred_element_type=jnp.float32)
            mixed = mixed / total
            o_ref[0] = jnp.where(position < window_extent, mixed, 0.0).astype(o_ref.dtype)

    keys_total = prompt_len + slots
    cost = pl.CostEstimate(
        flops=4 * items * rows * keys_total * HDIM,
        transcendentals=items * rows * keys_total,
        bytes_accessed=2 * (2 * items * rows * HDIM + 2 * items * keys_total * HDIM),
    )
    grid_spec = pltpu.PrefetchScalarGridSpec(
        num_scalar_prefetch=3,
        grid=(items, rows // tile),
        in_specs=[
            pl.BlockSpec((1, tile, HDIM), lambda i, b, g, n, h: (i, b, 0)),
            pl.BlockSpec((1, prompt_len, HDIM), lambda i, b, g, n, h: (g[i], 0, 0)),
            pl.BlockSpec((1, prompt_len, HDIM), lambda i, b, g, n, h: (g[i], 0, 0)),
            pl.BlockSpec((1, slots, HDIM), lambda i, b, g, n, h: (i, 0, h[0])),
            pl.BlockSpec((1, slots, HDIM), lambda i, b, g, n, h: (i, 0, h[0])),
        ],
        out_specs=pl.BlockSpec((1, tile, HDIM), lambda i, b, g, n, h: (i, b, 0)),
    )
    out = pl.pallas_call(
        kernel,
        grid_spec=grid_spec,
        out_shape=jax.ShapeDtypeStruct((items, rows, HDIM), jnp.bfloat16),
        compiler_params=pltpu.CompilerParams(vmem_limit_bytes=60 * 1024 * 1024),
        cost_estimate=cost,
    )(group.astype(jnp.int32), length.astype(jnp.int32), jnp.reshape(head, (1,)).astype(jnp.int32),
      queries, prompt_keys, prompt_values, resp_keys, resp_values)
    return out.reshape(items, slots, width)


def solution(mesh):
    placed = (
        P(None, "seq", None),
        P(None, "seq", None),
        P("resp", None, "seq"),
        P("resp", None, None),
        P("resp", None, None),
        P(None, "seq", "resp"),
        P(None, "resp", "seq"),
        P(None, "seq", None),
        P(None, "seq", None),
        P("resp", None, "seq"),
        P("resp", "seq", None),
        P("resp", None, None),
        P("resp", None, None),
        P(),
        P("resp"),
        P("resp"),
    )
    return jax.shard_map(
        body,
        mesh=mesh,
        in_specs=placed,
        out_specs=(P("resp", None, "seq"), P("resp", None, "seq"), P(None, "seq", "resp")),
        check_vma=False,
    )
```

profile of v0, /device:TPU:33, one launch (start us, length us, event | category | flops | bytes accessed | tf_op | source)
XLA Modules:
  0.0 366.0 jit_solution(13388169280110949714)
XLA Ops:
  17.5 6.8 %all-to-all-start = ((bf16[2,128,2048]{1,0,2:T(2,128)(2,1)}), bf16[2,128,2048]{1,0,2:T(2,128)(2,1)}, u32[]{:S(2)}, u32[]{:S(2)}) async-start(bf16[2,128,2048]{1,0,2:T(2,128)(2,1)} %bitcast.17), calls=%async_computation | async-start | bytes 2097152 | tf_op jit(solution)/shard_map/all_to_all | solution.py:161
  27.2 27.8 %all_gather.10 = f32[16,2,32]{2,1,0:T(2,128)S(1)} all-gather(f32[1,2,32]{2,1,0:T(2,128)S(1)} %maximum_exponential_fusion), channel_id=1, replica_groups=mesh['seq'=16,'resp'=8] {'seq'}, dimensions={0}, use_global_device_ids=true | all-gather | bytes 4352 | tf_op jit(solution)/shard_map/all_gather | solution.py:186
  60.4 4.1 %fusion.102 = (bf16[1,1024,1024]{2,1,0:T(8,128)(2,1)S(1)}, bf16[1,1024,1024]{2,1,0:T(8,128)(2,1)}) fusion(bf16[2,1024,1024]{2,1,0:T(8,128)(2,1)} %param.25), kind=kLoop, calls=%fused_computation.248 | loop fusion | bytes 8388608 | tf_op jit(solution)/shard_map/slice | solution.py:168
  64.5 6.3 %reshape.682 = bf16[8,128,16,64]{3,2,1,0:T(8,128)(2,1)} reshape(bf16[1,1024,1024]{2,1,0:T(8,128)(2,1)} %get-tuple-element.110) | data formatting | bytes 4194304 | tf_op jit(solution)/shard_map/reshape;squeeze | solution.py:76
  70.8 5.8 %copy.88 = bf16[8,128,16,64]{1,3,2,0:T(8,128)(2,1)} copy(bf16[8,128,16,64]{3,2,1,0:T(8,128)(2,1)} %reshape.682) | data formatting | bytes 4194304 | tf_op jit(solution)/shard_map/reshape;squeeze | solution.py:76
  79.7 3.9 %reshape.681 = bf16[8,128,16,64]{3,2,1,0:T(8,128)(2,1)} reshape(bf16[1,1024,1024]{2,1,0:T(8,128)(2,1)S(1)} %get-tuple-element.109) | data formatting | bytes 4194304 | tf_op jit(solution)/shard_map/reshape;squeeze | solution.py:76
  83.6 5.8 %copy.82 = bf16[8,128,16,64]{1,3,2,0:T(8,128)(2,1)S(1)} copy(bf16[8,128,16,64]{3,2,1,0:T(8,128)(2,1)} %reshape.681) | data formatting | bytes 4194304 | tf_op jit(solution)/shard_map/reshape;squeeze | solution.py:76
  120.7 3.0 fusion.1
  123.8 3.9 %fusion.3 = f32[8,16,8,8,128]{4,3,2,1,0:T(8,128)} fusion(f32[8,16,128,64]{2,3,1,0:T(8,128)S(1)} %fusion.1, f32[8,16,64,128]{3,2,1,0:T(8,128)S(1)} %fusion.50, bf16[8,128,128,1]{2,1,3,0:T(8,128)(2,1)S(1)} %bitcast.367, f32[8,128,16]{1,2,0:T(8,128)S(1)} %get-tuple-element.121), kind=kOutput, calls=%fused_computation.12 | convolution fusion | flops 1612709888 | bytes 12910592 | tf_op jit(solution)/shard_map/ctn,chpn->chtp/dot_general | solution.py:106
  127.7 2.8 broadcast_in_dim.201
  130.6 4.4 %all-to-all-start.1 = ((bf16[2,128,2048]{1,0,2:T(2,128)(2,1)}), bf16[2,128,2048]{1,0,2:T(2,128)(2,1)}, u32[]{:S(2)}, u32[]{:S(2)}) async-start(bf16[2,128,2048]{1,0,2:T(2,128)(2,1)} %bitcast.361), calls=%async_computation.1 | async-start | bytes 2097152 | tf_op jit(solution)/shard_map/all_to_all | solution.py:162
  135.2 4.3 %fusion = f32[8,16,128,64]{2,3,1,0:T(8,128)S(1)} fusion(f32[8,16,128]{2,1,0:T(8,128)S(1)} %bitcast.388, f32[8,128,128]{2,1,0:T(8,128)} %fusion.108, f32[8,16,128]{2,1,0:T(8,128)S(1)} %reduce_window_sum.42, pred[128,128]{1,0:T(8,128)(4,1)} %copy-done.33, bf16[8,128,16,64]{1,3,2,0:T(8,128)(2,1)S(1)} %copy.82), kind=kOutput, calls=%fused_computation.4 | convolution fusion | flops 278921216 | bytes 6963200 | tf_op jit(solution)/shard_map/chtu,chup->chtp/dot_general | solution.py:89
  139.5 4.0 %fusion.5 = f32[8,16,8,8,128]{4,3,2,1,0:T(8,128)} fusion(f32[8,16,128,64]{2,3,1,0:T(8,128)S(1)} %fusion, f32[8,16,64,128]{3,2,1,0:T(8,128)S(1)} %copy-done.3, bf16[8,128,128,1]{2,1,3,0:T(8,128)(2,1)S(1)} %bitcast.365, f32[8,128,16]{1,2,0:T(8,128)S(1)} %copy-done.17), kind=kOutput, calls=%fused_computation.16 | convolution fusion | flops 1612709888 | bytes 12910592 | tf_op jit(solution)/shard_map/ctn,chpn->chtp/dot_general | solution.py:106
  146.2 11.0 %all-to-all-done.1 = bf16[2,128,2048]{1,0,2:T(2,128)(2,1)} async-done(((bf16[2,128,2048]{1,0,2:T(2,128)(2,1)}), bf16[2,128,2048]{1,0,2:T(2,128)(2,1)}, u32[]{:S(2)}, u32[]{:S(2)}) %all-to-all-start.1) | async-done | bytes 1048608 | tf_op jit(solution)/shard_map/all_to_all | solution.py:162
  160.0 71.7 %all-gather.3.cloned.1.call-done = f32[32,32,64,128]{3,2,1,0:T(8,128)} async-done(((f32[2,32,64,128]{3,2,1,0:T(8,128)}), f32[32,32,64,128]{3,2,1,0:T(8,128)}) %all-gather.3.cloned.1.call-update) | async-done | bytes 33554448 | tf_op jit(solution)/shard_map/all_gather | solution.py:185
  231.7 13.6 %multiply_reduce_fusion = (f32[2,32,64,128]{3,2,1,0:T(8,128)S(1)}, f32[2,32,64,128]{3,2,1,0:T(8,128)S(1)}) fusion(f32[16,2,32,64,128]{4,3,2,1,0:T(8,128)} %bitcast.358, f32[16,2,32]{2,1,0:T(2,128)S(1)} %copy-done.27, f32[16,2,32]{2,1,0:T(2,128)S(1)} %copy-done.26), kind=kLoop, calls=%fused_computation | loop fusion | flops 32505856 | bytes 37756928 | tf_op jit(solution)/shard_map/reduce_sum | solution.py:195
  246.4 4.4 %reshape.662.q_ref = bf16[2,4096,128]{2,1,0:T(8,128)(2,1)} reshape(bf16[2,1024,512]{2,1,0:T(8,128)(2,1)} %param.18) | data formatting | bytes 4194304 | tf_op jit(solution)/shard_map/reshape | solution.py:242
  255.6 76.0 %shard_map.175 = bf16[2,4096,128]{2,1,0:T(8,128)(2,1)} custom-call(s32[2]{0:T(128)} %group_ref.1, s32[2]{0:T(128)} %len_ref.1, s32[1]{0:T(128)} %bitcast.head_ref, bf16[2,4096,128]{2,1,0:T(8,128)(2,1)} %reshape.662.q_ref, bf16[2,2048,128]{2,1,0:T(8,128)(2,1)} %bitcast.380, bf16[2,2048,128]{2,1,0:T(8,128)(2,1)} %bitcast.381, bf16[2,1024,1024]{2,1,0:T(8,128)(2,1)} %rk_ref.1, ...), custom_call_target="tpu_custom_call" | custom-call | flops 12884901888 | bytes 7340032 | tf_op jit(solution)/shard_map/pallas_call | solution.py:296
  331.6 4.7 %reshape.665 = bf16[2,1024,512]{2,1,0:T(8,128)(2,1)} reshape(bf16[2,4096,128]{2,1,0:T(8,128)(2,1)} %shard_map.175) | data formatting | bytes 4194304 | tf_op jit(solution)/shard_map/reshape | solution.py:304
  337.9 4.6 %multiply_reduce_fusion.2 = (f32[1024,16]{0,1:T(8,128)S(1)}, f32[1024,16,64]{0,2,1:T(8,128)S(1)}) fusion(bf16[2,1024,128]{2,1,0:T(8,128)(2,1)S(1)} %copy-done.6, f32[2,16,64,128]{3,2,1,0:T(8,128)} %all-reduce.2.cloned.1.call-done, s32[]{:T(128)S(6)} %select_n.100, f32[1024,16]{0,1:T(8,128)S(1)} %copy-done.16, f32[8,16,8,8,128]{4,3,2,1,0:T(8,128)} %fusion.3), kind=kOutput, calls=%fused_computation.18 | convolution fusion | flops 1614790656 | bytes 9306116 | tf_op jit(solution)/shard_map/tn,hdn->thd/dot_general | solution.py:218
  343.2 2.6 copy.91
  345.8 4.6 %multiply_reduce_fusion.3 = (f32[1024,16]{0,1:T(8,128)S(1)}, f32[1024,16,64]{0,2,1:T(8,128)S(1)}) fusion(bf16[2,1024,128]{2,1,0:T(8,128)(2,1)S(1)} %copy-done.6, f32[2,16,64,128]{3,2,1,0:T(8,128)} %all-reduce.2.cloned.1.call-done, s32[]{:T(128)S(6)} %select_n.97, f32[1024,16]{0,1:T(8,128)S(1)} %copy-done.15, f32[8,16,8,8,128]{4,3,2,1,0:T(8,128)} %fusion.5), kind=kOutput, calls=%fused_computation.25 | convolution fusion | flops 1614790656 | bytes 9306116 | tf_op jit(solution)/shard_map/tn,hdn->thd/dot_general | solution.py:218
  351.1 2.6 copy.85
  356.3 2.4 pad_maximum_fusion
  (191 shorter events, 66.2 us)
Async XLA Ops:
  7.2 6.0 %copy-start.18 = (bf16[2,128,128]{2,1,0:T(8,128)(2,1)S(1)}, bf16[2,128,128]{2,1,0:T(8,128)(2,1)}, u32[]{:S(2)}) copy-start(bf16[2,128,128]{2,1,0:T(8,128)(2,1)} %param.23) | copy-start | bytes 196612
  7.2 224.5 %all-gather.3.cloned.1.call-start = ((), (), s32[]{:S(2)}) async-start(), calls=%async_computation.3 | async-start | bytes 35651584 | tf_op jit(solution)/shard_map/all_gather | solution.py:185
  15.2 9.1 %copy-start.35 = (s32[2]{0:T(128)S(1)}, s32[2]{0:T(128)}, u32[]{:S(2)}) copy-start(s32[2]{0:T(128)} %group_ref.1) | copy-start | bytes 28
  15.2 40.3 %copy-start.13 = (bf16[2,128,1024]{2,1,0:T(8,128)(2,1)S(1)}, bf16[2,128,1024]{2,1,0:T(8,128)(2,1)}, u32[]{:S(2)}) copy-start(bf16[2,128,1024]{2,1,0:T(8,128)(2,1)} %param.17) | copy-start | bytes 1572868
  15.2 41.4 %copy-start.38 = (f32[256]{0:T(256)S(1)}, f32[256]{0:T(256)}, u32[]{:S(2)}) copy-start(f32[256]{0:T(256)} %param.29) | copy-start | bytes 3076
  15.2 41.5 %copy-start.25 = (f32[2,16,1024]{2,1,0:T(8,128)S(1)}, f32[2,16,1024]{2,1,0:T(8,128)}, u32[]{:S(2)}) copy-start(f32[2,16,1024]{2,1,0:T(8,128)} %param.26) | copy-start | bytes 393220
  17.5 110.2 %all-to-all-start = ((bf16[2,128,2048]{1,0,2:T(2,128)(2,1)}), bf16[2,128,2048]{1,0,2:T(2,128)(2,1)}, u32[]{:S(2)}, u32[]{:S(2)}) async-start(bf16[2,128,2048]{1,0,2:T(2,128)(2,1)} %bitcast.17), calls=%async_computation | async-start | bytes 2097152 | tf_op jit(solution)/shard_map/all_to_all | solution.py:161
  83.6 16.4 %copy-start.30 = (f32[16,2,32]{2,0,1:T(8,128)S(1)}, f32[16,2,32]{2,0,1:T(8,128)}, u32[]{:S(2)}) copy-start(f32[16,2,32]{2,0,1:T(8,128)} %copy.71) | copy-start | bytes 12292
  83.6 19.9 %copy-start.14 = (f32[2,32,128]{2,1,0:T(8,128)S(1)}, f32[2,32,128]{2,1,0:T(8,128)}, u32[]{:S(2)}) copy-start(f32[2,32,128]{2,1,0:T(8,128)} %param.22) | copy-start | bytes 98308
  83.6 19.9 %copy-start.9 = (bf16[2,128,128]{2,1,0:T(8,128)(2,1)S(1)}, bf16[2,128,128]{2,1,0:T(8,128)(2,1)}, u32[]{:S(2)}) copy-start(bf16[2,128,128]{2,1,0:T(8,128)(2,1)} %param.24) | copy-start | bytes 196612
  83.6 26.6 %copy-start.5 = (bf16[2,1024,128]{2,1,0:T(8,128)(2,1)S(1)}, bf16[2,1024,128]{2,1,0:T(8,128)(2,1)}, u32[]{:S(2)}) copy-start(bf16[2,1024,128]{2,1,0:T(8,128)(2,1)} %param.28) | copy-start | bytes 1572868
  89.6 10.4 %copy-start.32 = (f32[8,16]{1,0:T(8,128)}, f32[8,16]{1,0:T(8,128)S(1)}, u32[]{:S(2)}) copy-start(f32[8,16]{1,0:T(8,128)S(1)} %slice_reduce_fusion.1) | copy-start | bytes 1540
  96.2 16.5 %copy-start = (bf16[8,128,16,64]{1,3,2,0:T(8,128)(2,1)S(1)}, bf16[8,128,16,64]{1,3,2,0:T(8,128)(2,1)}, u32[]{:S(2)}) copy-start(bf16[8,128,16,64]{1,3,2,0:T(8,128)(2,1)} %copy.88) | copy-start | bytes 6291460
  100.0 20.7 %copy-start.33 = (pred[128,128]{1,0:T(8,128)(4,1)}, pred[128,128]{1,0:T(8,128)(4,1)S(1)}, u32[]{:S(2)}) copy-start(pred[128,128]{1,0:T(8,128)(4,1)S(1)} %iota_compare_fusion) | copy-start | bytes 49156
  123.7 11.5 %copy-start.28 = (f32[16,8,128]{2,0,1:T(8,128)S(1)}, f32[16,8,128]{2,0,1:T(8,128)}, u32[]{:S(2)}) copy-start(f32[16,8,128]{2,0,1:T(8,128)} %copy.127) | copy-start | bytes 196612
  130.6 26.7 %all-to-all-start.1 = ((bf16[2,128,2048]{1,0,2:T(2,128)(2,1)}), bf16[2,128,2048]{1,0,2:T(2,128)(2,1)}, u32[]{:S(2)}, u32[]{:S(2)}) async-start(bf16[2,128,2048]{1,0,2:T(2,128)(2,1)} %bitcast.361), calls=%async_computation.1 | async-start | bytes 2097152 | tf_op jit(solution)/shard_map/all_to_all | solution.py:162
  134.9 203.0 %all-reduce.2.cloned.1.call-start = ((), (), s32[]{:S(2)}) async-start(), calls=%async_computation.2 | async-start | bytes 2097152 | tf_op jit(solution)/shard_map/psum | solution.py:27
  143.5 88.2 %copy-start.26 = (f32[16,2,32]{2,1,0:T(2,128)S(1)}, f32[16,2,32]{2,1,0:T(2,128)}, u32[]{:S(2)}) copy-start(f32[16,2,32]{2,1,0:T(2,128)} %get-tuple-element.84) | copy-start | bytes 12292
  143.5 88.2 %copy-start.27 = (f32[16,2,32]{2,1,0:T(2,128)S(1)}, f32[16,2,32]{2,1,0:T(2,128)}, u32[]{:S(2)}) copy-start(f32[16,2,32]{2,1,0:T(2,128)} %broadcast_select_fusion.1) | copy-start | bytes 12292
  246.4 5.5 %copy-start.11 = (bf16[2,128,128]{2,1,0:T(8,128)(2,1)S(1)}, bf16[2,128,128]{2,1,0:T(8,128)(2,1)}, u32[]{:S(2)}) copy-start(bf16[2,128,128]{2,1,0:T(8,128)(2,1)} %param.24) | copy-start | bytes 196612
  246.4 5.5 %copy-start.20 = (f32[128,32]{0,1:T(8,128)S(1)}, f32[128,32]{0,1:T(8,128)}, u32[]{:S(2)}) copy-start(f32[128,32]{0,1:T(8,128)} %get-tuple-element.129) | copy-start | bytes 49156
  331.5 4.9 %copy-start.4 = (f32[128,32,64]{0,2,1:T(8,128)S(1)}, f32[128,32,64]{0,2,1:T(8,128)}, u32[]{:S(2)}) copy-start(f32[128,32,64]{0,2,1:T(8,128)} %get-tuple-element.158) | copy-start | bytes 3145732
  331.6 6.4 %copy-start.6 = (bf16[2,1024,128]{2,1,0:T(8,128)(2,1)S(1)}, bf16[2,1024,128]{2,1,0:T(8,128)(2,1)}, u32[]{:S(2)}) copy-start(bf16[2,1024,128]{2,1,0:T(8,128)(2,1)} %param.28) | copy-start | bytes 1572868
  331.6 6.4 %copy-start.16 = (f32[1024,16]{0,1:T(8,128)S(1)}, f32[1024,16]{0,1:T(8,128)}, u32[]{:S(2)}) copy-start(f32[1024,16]{0,1:T(8,128)} %bitcast_bitcast_fusion) | copy-start | bytes 196612
  (19 other events, 51.0 us)
Sparse Core Ops, SparseCore 0:
  15.4 216.2 all-gather.2
  252.0 58.8 all-reduce.1
where the time goes:
time: 372 us; the launch traced here: 366 us
  waiting for transfers between devices  82.8 us (22%)
  Pallas kernels  76 us (20%)
  local copies, waits for them, and re-layouts  67.2 us (18%)
  other arithmetic  45.1 us (12%)
  matrix products  37.1 us (10%)
  blocking collectives  27.8 us (7%)
  between operations  18.7 us (5%)
  starting transfers between devices  11.5 us (3%)
    pallas_call x1, Pallas kernels, response_attention(): pl.pallas_call(kernel, grid_spec=grid_spec, out_shape=jax.ShapeDtypeStruc...  76 us
    all_gather x1, waiting for transfers between devices, body(): gathered_states = lax.all_gather(local_state, 'seq')  71.7 us
    all_gather x1, blocking collectives, body(): gathered_decays = lax.all_gather(decay_total, 'seq')  27.8 us
    another operation x4, local copies, waits for them, and re-layouts, chunked_pass(): xs = inputs.reshape(blocks, QS, heads, SP).transpose(0, 2, 1, 3)  21.9 us
    reduce_sum x1, other arithmetic, body(): jnp.sum(before_weights[:, :, :, None, None] * gathered_states, axis=0)  13.6 us
    all_to_all x1, waiting for transfers between devices, body(): lax.all_to_all(spread_values, 'seq', split_axis=2, concat_axis=1, tiled=T...  11 us
    dot_general x2, matrix products, body(): jnp.einsum('tn,hdn->thd', resp_c[item].astype(jnp.float32), initial, prec...  9.28 us
    dot_general x2, matrix products, chunked_pass(): jnp.einsum('ctn,chpn->chtp', cs.astype(jnp.float32), before, precision=la...  7.92 us
  transfers between devices with their start and end apart: 4, of which 2 were waited for; matrix products, arithmetic and copies ran while one was open for 27% of the time, Pallas kernels for 21%

commit v1 on v0

--- a/solution.py
+++ b/solution.py
@@ -183,7 +183,14 @@
     local_state = jnp.stack(local_states)
     decay_total = jnp.exp(jnp.stack(log_totals))
     gathered_states = lax.all_gather(local_state, "seq")
-    gathered_decays = lax.all_gather(decay_total, "seq")
+    slot = lax.broadcasted_iota(jnp.int32, (seq_count,) + decay_total.shape, 0)
+    gathered_decays = lax.psum(jnp.where(slot == seq_index, decay_total[None], 0.0), "seq")
+    heads_here = resp_query.shape[2] // HDIM
+    own_head = seq_index // repeat
+    resp_attn_out = response_attention(
+        resp_query, moved_keys, moved_values, resp_keys, resp_values, resp_group, resp_len, own_head
+    )
+    gathered_states, resp_attn_out = lax.optimization_barrier((gathered_states, resp_attn_out))
     shard = lax.broadcasted_iota(jnp.int32, (seq_count, seq_count), 0)
     later = lax.broadcasted_iota(jnp.int32, (seq_count, seq_count), 1)
     between = (later > shard) & (later < seq_index)
@@ -208,7 +215,6 @@
     finals = inclusive
     ratio = seq_count // lax.axis_size("resp")
     piece = lax.dynamic_slice_in_dim(finals, seq_index % ratio * resp_heads, resp_heads, 1)
-    piece, resp_query = lax.optimization_barrier((piece, resp_query))
     start_states = broadcast(piece, "resp", seq_index // ratio)
     positions = lax.broadcasted_iota(jnp.int32, (slots,), 0)
     resp_outs = []
@@ -225,11 +231,6 @@
         valid = positions < resp_len[item]
         resp_outs.append(jnp.where(valid[:, None], head_norm(corrected), 0.0).astype(jnp.bfloat16))
     resp_ssm_out = jnp.stack(resp_outs)
-    heads_here = resp_query.shape[2] // HDIM
-    own_head = seq_index // repeat
-    resp_attn_out = response_attention(
-        resp_query, moved_keys, moved_values, resp_keys, resp_values, resp_group, resp_len, own_head
-    )
     return (resp_attn_out, resp_ssm_out, prompt_ssm_out)
 
 

time: 372 us -> 397 us (1.067)
  blocking collectives: 27.8 us -> 62.2 us
  Pallas kernels: 76 us -> 56.7 us
  waiting for transfers between devices: 82.8 us -> 94.5 us
    psum x1, waiting for transfers between devices: 0.01 us -> 86.1 us  [broadcast(): return lax.psum(kept, axis)]
    all_gather x1, waiting for transfers between devices: 71.7 us -> 0.01 us  [body(): gathered_states = lax.all_gather(local_state, 'seq')]
    psum x0 -> x1, blocking collectives: none -> 62.2 us  [body(): lax.psum(jnp.where(slot == seq_index, decay_total[None], 0.0), 'seq')]
    all_gather x1 -> x0, blocking collectives: 27.8 us -> none  [body(): gathered_decays = lax.all_gather(decay_total, 'seq')]
    pallas_call x1, Pallas kernels: 76 us -> 56.7 us  [response_attention(): pl.pallas_call(kernel, grid_spec=grid_spec, out_shape=jax.ShapeDtypeStruc...]
  transfers between devices with their start and end apart: 4 -> 4, of which waited for: 2 -> 2; matrix products, arithmetic and copies ran while one was open for 27% -> 26% of each run, Pallas kernels for 21% -> 14%
where the time goes in v1:
time: 397 us; the launch traced here: 393 us
  waiting for transfers between devices  94.5 us (24%)
  local copies, waits for them, and re-layouts  64.7 us (16%)
  blocking collectives  62.2 us (16%)
  Pallas kernels  56.7 us (14%)
  other arithmetic  46.9 us (12%)
  matrix products  37.1 us (9%)
  between operations  19.1 us (5%)
  starting transfers between devices  11.6 us (3%)
    psum x1, waiting for transfers between devices, broadcast(): return lax.psum(kept, axis)  86.1 us
    psum x1, blocking collectives, body(): lax.psum(jnp.where(slot == seq_index, decay_total[None], 0.0), 'seq')  62.2 us
    pallas_call x1, Pallas kernels, response_attention(): pl.pallas_call(kernel, grid_spec=grid_spec, out_shape=jax.ShapeDtypeStruc...  56.7 us
    another operation x4, local copies, waits for them, and re-layouts, chunked_pass(): xs = inputs.reshape(blocks, QS, heads, SP).transpose(0, 2, 1, 3)  21.4 us
    reduce_sum x1, other arithmetic, body(): jnp.sum(before_weights[:, :, :, None, None] * gathered_states, axis=0)  13.9 us
    dot_general x2, matrix products, body(): jnp.einsum('tn,hdn->thd', resp_c[item].astype(jnp.float32), initial, prec...  9.27 us
    all_to_all x1, waiting for transfers between devices, body(): lax.all_to_all(spread_values, 'seq', split_axis=2, concat_axis=1, tiled=T...  8.36 us
  transfers between devices with their start and end apart: 4, of which 2 were waited for; matrix products, arithmetic and copies ran while one was open for 26% of the time, Pallas kernels for 14%

profile of v1, /device:TPU:33, one launch (start us, length us, event | category | flops | bytes accessed | tf_op | source)
XLA Modules:
  0.0 392.7 jit_solution(18241170073779835473)
XLA Ops:
  18.5 6.9 %all-to-all-start = ((bf16[2,128,2048]{1,0,2:T(2,128)(2,1)}), bf16[2,128,2048]{1,0,2:T(2,128)(2,1)}, u32[]{:S(2)}, u32[]{:S(2)}) async-start(bf16[2,128,2048]{1,0,2:T(2,128)(2,1)} %bitcast.17), calls=%async_computation | async-start | bytes 2097152 | tf_op jit(solution)/shard_map/all_to_all | solution.py:161
  28.6 2.6 reshape.648.q_ref
  32.4 62.2 %psum.14 = f32[16,2,32]{2,1,0:T(2,128)S(1)} all-reduce(f32[16,2,32]{2,1,0:T(2,128)S(1)} %broadcast_select_fusion.1), channel_id=1, replica_groups=mesh['seq'=16,'resp'=8] {'seq'}, use_global_device_ids=true, to_apply=%region_3.4 | all-reduce | flops 1024 | bytes 8192 | tf_op jit(solution)/shard_map/psum | solution.py:187
  98.9 4.2 %fusion.102 = (bf16[1,1024,1024]{2,1,0:T(8,128)(2,1)S(1)}, bf16[1,1024,1024]{2,1,0:T(8,128)(2,1)}) fusion(bf16[2,1024,1024]{2,1,0:T(8,128)(2,1)} %param.25), kind=kLoop, calls=%fused_computation.249 | loop fusion | bytes 8388608 | tf_op jit(solution)/shard_map/slice | solution.py:168
  103.1 6.4 %reshape.668 = bf16[8,128,16,64]{3,2,1,0:T(8,128)(2,1)} reshape(bf16[1,1024,1024]{2,1,0:T(8,128)(2,1)} %get-tuple-element.110) | data formatting | bytes 4194304 | tf_op jit(solution)/shard_map/reshape;squeeze | solution.py:76
  109.5 5.8 %copy.88 = bf16[8,128,16,64]{1,3,2,0:T(8,128)(2,1)} copy(bf16[8,128,16,64]{3,2,1,0:T(8,128)(2,1)} %reshape.668) | data formatting | bytes 4194304 | tf_op jit(solution)/shard_map/reshape;squeeze | solution.py:76
  118.3 3.9 %reshape.667 = bf16[8,128,16,64]{3,2,1,0:T(8,128)(2,1)} reshape(bf16[1,1024,1024]{2,1,0:T(8,128)(2,1)S(1)} %get-tuple-element.109) | data formatting | bytes 4194304 | tf_op jit(solution)/shard_map/reshape;squeeze | solution.py:76
  122.3 5.3 %copy.81 = bf16[8,128,16,64]{1,3,2,0:T(8,128)(2,1)S(1)} copy(bf16[8,128,16,64]{3,2,1,0:T(8,128)(2,1)} %reshape.667) | data formatting | bytes 4194304 | tf_op jit(solution)/shard_map/reshape;squeeze | solution.py:76
  159.4 3.0 fusion.1
  162.4 3.9 %fusion.3 = f32[8,16,8,8,128]{4,3,2,1,0:T(8,128)} fusion(f32[8,16,128,64]{2,3,1,0:T(8,128)S(1)} %fusion.1, f32[8,16,64,128]{3,2,1,0:T(8,128)S(1)} %fusion.50, bf16[8,128,128,1]{2,1,3,0:T(8,128)(2,1)S(1)} %bitcast.367, f32[8,128,16]{1,2,0:T(8,128)S(1)} %get-tuple-element.121), kind=kOutput, calls=%fused_computation.12 | convolution fusion | flops 1612709888 | bytes 12910592 | tf_op jit(solution)/shard_map/ctn,chpn->chtp/dot_general | solution.py:106
  166.4 2.9 broadcast_in_dim.209
  169.2 4.3 %all-to-all-start.1 = ((bf16[2,128,2048]{1,0,2:T(2,128)(2,1)}), bf16[2,128,2048]{1,0,2:T(2,128)(2,1)}, u32[]{:S(2)}, u32[]{:S(2)}) async-start(bf16[2,128,2048]{1,0,2:T(2,128)(2,1)} %bitcast.361), calls=%async_computation.1 | async-start | bytes 2097152 | tf_op jit(solution)/shard_map/all_to_all | solution.py:162
  173.8 4.2 %fusion = f32[8,16,128,64]{2,3,1,0:T(8,128)S(1)} fusion(f32[8,16,128]{2,1,0:T(8,128)S(1)} %bitcast.388, f32[8,128,128]{2,1,0:T(8,128)} %fusion.108, f32[8,16,128]{2,1,0:T(8,128)S(1)} %reduce_window_sum.42, pred[128,128]{1,0:T(8,128)(4,1)} %copy-done.32, bf16[8,128,16,64]{1,3,2,0:T(8,128)(2,1)S(1)} %copy.81), kind=kOutput, calls=%fused_computation.4 | convolution fusion | flops 278921216 | bytes 6963200 | tf_op jit(solution)/shard_map/chtu,chup->chtp/dot_general | solution.py:89
  178.1 4.0 %fusion.5 = f32[8,16,8,8,128]{4,3,2,1,0:T(8,128)} fusion(f32[8,16,128,64]{2,3,1,0:T(8,128)S(1)} %fusion, f32[8,16,64,128]{3,2,1,0:T(8,128)S(1)} %copy-done.3, bf16[8,128,128,1]{2,1,3,0:T(8,128)(2,1)S(1)} %bitcast.365, f32[8,128,16]{1,2,0:T(8,128)S(1)} %copy-done.16), kind=kOutput, calls=%fused_computation.16 | convolution fusion | flops 1612709888 | bytes 12910592 | tf_op jit(solution)/shard_map/ctn,chpn->chtp/dot_general | solution.py:106
  184.8 8.4 %all-to-all-done.1 = bf16[2,128,2048]{1,0,2:T(2,128)(2,1)} async-done(((bf16[2,128,2048]{1,0,2:T(2,128)(2,1)}), bf16[2,128,2048]{1,0,2:T(2,128)(2,1)}, u32[]{:S(2)}, u32[]{:S(2)}) %all-to-all-start.1) | async-done | bytes 1048608 | tf_op jit(solution)/shard_map/all_to_all | solution.py:162
  195.9 56.7 %shard_map.175 = bf16[2,4096,128]{2,1,0:T(8,128)(2,1)} custom-call(s32[2]{0:T(128)} %group_ref.1, s32[2]{0:T(128)} %len_ref.1, s32[1]{0:T(128)} %bitcast.15.head_ref, bf16[2,4096,128]{2,1,0:T(8,128)(2,1)} %reshape.648.q_ref, bf16[2,2048,128]{2,1,0:T(8,128)(2,1)} %bitcast.380, bf16[2,2048,128]{2,1,0:T(8,128)(2,1)} %bitcast.381, ...), custom_call_target="tpu_custom_call" | custom-call | flops 12884901888 | bytes 7340032 | tf_op jit(solution)/shard_map/pallas_call | solution.py:297
  252.5 4.4 %reshape.651 = bf16[2,1024,512]{2,1,0:T(8,128)(2,1)} reshape(bf16[2,4096,128]{2,1,0:T(8,128)(2,1)} %shard_map.175) | data formatting | bytes 4194304 | tf_op jit(solution)/shard_map/reshape | solution.py:305
  256.9 13.9 %multiply_reduce_fusion = (f32[2,32,64,128]{3,2,1,0:T(8,128)S(1)}, f32[2,32,64,128]{3,2,1,0:T(8,128)S(1)}) fusion(f32[16,2,32,64,128]{4,3,2,1,0:T(8,128)} %bitcast.358, f32[16,2,32]{2,1,0:T(2,128)S(1)} %copy-done.26, f32[16,2,32]{2,1,0:T(2,128)S(1)} %copy-done.25), kind=kLoop, calls=%fused_computation | loop fusion | flops 32505856 | bytes 37756928 | tf_op jit(solution)/shard_map/reduce_sum | solution.py:202
  278.5 86.1 %all-reduce.2.cloned.1.call-done = f32[2,16,64,128]{3,2,1,0:T(8,128)} async-done(((f32[2,16,64,128]{3,2,1,0:T(8,128)}), f32[2,16,64,128]{3,2,1,0:T(8,128)}) %all-reduce.2.cloned.1.call-update) | async-done | bytes 1048592 | tf_op jit(solution)/shard_map/psum | solution.py:27
  364.6 4.6 %multiply_reduce_fusion.2 = (f32[1024,16]{0,1:T(8,128)S(1)}, f32[1024,16,64]{0,2,1:T(8,128)S(1)}) fusion(bf16[2,1024,128]{2,1,0:T(8,128)(2,1)S(1)} %copy-done.5, f32[2,16,64,128]{3,2,1,0:T(8,128)} %all-reduce.2.cloned.1.call-done, s32[]{:T(128)S(6)} %select_n.105, f32[1024,16]{0,1:T(8,128)S(1)} %copy-done.15, f32[8,16,8,8,128]{4,3,2,1,0:T(8,128)} %fusion.3), kind=kOutput, calls=%fused_computation.18 | convolution fusion | flops 1614790656 | bytes 9306116 | tf_op jit(solution)/shard_map/tn,hdn->thd/dot_general | solution.py:224
  369.9 2.6 copy.91
  372.5 4.6 %multiply_reduce_fusion.3 = (f32[1024,16]{0,1:T(8,128)S(1)}, f32[1024,16,64]{0,2,1:T(8,128)S(1)}) fusion(bf16[2,1024,128]{2,1,0:T(8,128)(2,1)S(1)} %copy-done.5, f32[2,16,64,128]{3,2,1,0:T(8,128)} %all-reduce.2.cloned.1.call-done, s32[]{:T(128)S(6)} %select_n.102, f32[1024,16]{0,1:T(8,128)S(1)} %copy-done.14, f32[8,16,8,8,128]{4,3,2,1,0:T(8,128)} %fusion.5), kind=kOutput, calls=%fused_computation.25 | convolution fusion | flops 1614790656 | bytes 9306116 | tf_op jit(solution)/shard_map/tn,hdn->thd/dot_general | solution.py:224
  377.8 2.6 copy.85
  383.0 2.4 pad_maximum_fusion
  (190 shorter events, 67.8 us)
Async XLA Ops:
  7.2 6.0 %copy-start.17 = (bf16[2,128,128]{2,1,0:T(8,128)(2,1)S(1)}, bf16[2,128,128]{2,1,0:T(8,128)(2,1)}, u32[]{:S(2)}) copy-start(bf16[2,128,128]{2,1,0:T(8,128)(2,1)} %param.23) | copy-start | bytes 196612
  7.2 249.7 %all-gather.3.cloned.1.call-start = ((), (), s32[]{:S(2)}) async-start(), calls=%async_computation.3 | async-start | bytes 35651584 | tf_op jit(solution)/shard_map/all_gather | solution.py:185
  15.2 10.3 %copy-start.34 = (s32[2]{0:T(128)S(1)}, s32[2]{0:T(128)}, u32[]{:S(2)}) copy-start(s32[2]{0:T(128)} %group_ref.1) | copy-start | bytes 28
  15.2 13.4 %copy-start.6 = (bf16[2,1024,512]{2,1,0:T(8,128)(2,1)S(1)}, bf16[2,1024,512]{2,1,0:T(8,128)(2,1)}, u32[]{:S(2)}) copy-start(bf16[2,1024,512]{2,1,0:T(8,128)(2,1)} %param.18) | copy-start | bytes 6291460
  16.7 78.5 %copy-start.37 = (f32[256]{0:T(256)S(1)}, f32[256]{0:T(256)}, u32[]{:S(2)}) copy-start(f32[256]{0:T(256)} %param.29) | copy-start | bytes 3076
  16.7 78.5 %copy-start.24 = (f32[2,16,1024]{2,1,0:T(8,128)S(1)}, f32[2,16,1024]{2,1,0:T(8,128)}, u32[]{:S(2)}) copy-start(f32[2,16,1024]{2,1,0:T(8,128)} %param.26) | copy-start | bytes 393220
  18.5 12.7 %copy-start.12 = (bf16[2,128,1024]{2,1,0:T(8,128)(2,1)S(1)}, bf16[2,128,1024]{2,1,0:T(8,128)(2,1)}, u32[]{:S(2)}) copy-start(bf16[2,128,1024]{2,1,0:T(8,128)(2,1)} %param.17) | copy-start | bytes 1572868
  18.5 147.9 %all-to-all-start = ((bf16[2,128,2048]{1,0,2:T(2,128)(2,1)}), bf16[2,128,2048]{1,0,2:T(2,128)(2,1)}, u32[]{:S(2)}, u32[]{:S(2)}) async-start(bf16[2,128,2048]{1,0,2:T(2,128)(2,1)} %bitcast.17), calls=%async_computation | async-start | bytes 2097152 | tf_op jit(solution)/shard_map/all_to_all | solution.py:161
  122.2 16.4 %copy-start.29 = (f32[16,2,32]{2,0,1:T(8,128)S(1)}, f32[16,2,32]{2,0,1:T(8,128)}, u32[]{:S(2)}) copy-start(f32[16,2,32]{2,0,1:T(8,128)} %copy.84) | copy-start | bytes 12292
  122.2 19.9 %copy-start.13 = (f32[2,32,128]{2,1,0:T(8,128)S(1)}, f32[2,32,128]{2,1,0:T(8,128)}, u32[]{:S(2)}) copy-start(f32[2,32,128]{2,1,0:T(8,128)} %param.22) | copy-start | bytes 98308
  122.2 19.9 %copy-start.9 = (bf16[2,128,128]{2,1,0:T(8,128)(2,1)S(1)}, bf16[2,128,128]{2,1,0:T(8,128)(2,1)}, u32[]{:S(2)}) copy-start(bf16[2,128,128]{2,1,0:T(8,128)(2,1)} %param.24) | copy-start | bytes 196612
  122.2 26.6 %copy-start.4 = (bf16[2,1024,128]{2,1,0:T(8,128)(2,1)S(1)}, bf16[2,1024,128]{2,1,0:T(8,128)(2,1)}, u32[]{:S(2)}) copy-start(bf16[2,1024,128]{2,1,0:T(8,128)(2,1)} %param.28) | copy-start | bytes 1572868
  127.7 11.0 %copy-start.31 = (f32[8,16]{1,0:T(8,128)}, f32[8,16]{1,0:T(8,128)S(1)}, u32[]{:S(2)}) copy-start(f32[8,16]{1,0:T(8,128)S(1)} %slice_reduce_fusion.1) | copy-start | bytes 1540
  134.6 16.8 %copy-start = (bf16[8,128,16,64]{1,3,2,0:T(8,128)(2,1)S(1)}, bf16[8,128,16,64]{1,3,2,0:T(8,128)(2,1)}, u32[]{:S(2)}) copy-start(bf16[8,128,16,64]{1,3,2,0:T(8,128)(2,1)} %copy.88) | copy-start | bytes 6291460
  138.6 20.7 %copy-start.32 = (pred[128,128]{1,0:T(8,128)(4,1)}, pred[128,128]{1,0:T(8,128)(4,1)S(1)}, u32[]{:S(2)}) copy-start(pred[128,128]{1,0:T(8,128)(4,1)S(1)} %iota_compare_fusion) | copy-start | bytes 49156
  162.4 11.4 %copy-start.27 = (f32[16,8,128]{2,0,1:T(8,128)S(1)}, f32[16,8,128]{2,0,1:T(8,128)}, u32[]{:S(2)}) copy-start(f32[16,8,128]{2,0,1:T(8,128)} %copy.127) | copy-start | bytes 196612
  169.2 24.0 %all-to-all-start.1 = ((bf16[2,128,2048]{1,0,2:T(2,128)(2,1)}), bf16[2,128,2048]{1,0,2:T(2,128)(2,1)}, u32[]{:S(2)}, u32[]{:S(2)}) async-start(bf16[2,128,2048]{1,0,2:T(2,128)(2,1)} %bitcast.361), calls=%async_computation.1 | async-start | bytes 2097152 | tf_op jit(solution)/shard_map/all_to_all | solution.py:162
  173.6 191.0 %all-reduce.2.cloned.1.call-start = ((), (), s32[]{:S(2)}) async-start(), calls=%async_computation.2 | async-start | bytes 2097152 | tf_op jit(solution)/shard_map/psum | solution.py:27
  252.5 4.4 %copy-start.26 = (f32[16,2,32]{2,1,0:T(2,128)S(1)}, f32[16,2,32]{2,1,0:T(2,128)}, u32[]{:S(2)}) copy-start(f32[16,2,32]{2,1,0:T(2,128)} %broadcast_select_fusion) | copy-start | bytes 12292
  256.9 15.0 %copy-start.11 = (bf16[2,128,128]{2,1,0:T(8,128)(2,1)S(1)}, bf16[2,128,128]{2,1,0:T(8,128)(2,1)}, u32[]{:S(2)}) copy-start(bf16[2,128,128]{2,1,0:T(8,128)(2,1)} %param.24) | copy-start | bytes 196612
  256.9 15.0 %copy-start.19 = (f32[128,32]{0,1:T(8,128)S(1)}, f32[128,32]{0,1:T(8,128)}, u32[]{:S(2)}) copy-start(f32[128,32]{0,1:T(8,128)} %get-tuple-element.129) | copy-start | bytes 49156
  275.5 89.1 %copy-start.5 = (bf16[2,1024,128]{2,1,0:T(8,128)(2,1)S(1)}, bf16[2,1024,128]{2,1,0:T(8,128)(2,1)}, u32[]{:S(2)}) copy-start(bf16[2,1024,128]{2,1,0:T(8,128)(2,1)} %param.28) | copy-start | bytes 1572868
  275.5 89.1 %copy-start.15 = (f32[1024,16]{0,1:T(8,128)S(1)}, f32[1024,16]{0,1:T(8,128)}, u32[]{:S(2)}) copy-start(f32[1024,16]{0,1:T(8,128)} %bitcast_bitcast_fusion) | copy-start | bytes 196612
  377.8 4.8 %copy-start.36 = (pred[1024]{0:T(1024)(128)(4,1)S(1)}, pred[1024]{0:T(1024)(128)(4,1)}, u32[]{:S(2)}) copy-start(pred[1024]{0:T(1024)(128)(4,1)} %iota_compare_fusion.3) | copy-start | bytes 3076
  (18 other events, 48.8 us)
Sparse Core Ops, SparseCore 0:
  15.3 218.3 all-gather.2
  272.0 92.5 all-reduce.1

commit v2 on v1

--- a/solution.py
+++ b/solution.py
@@ -167,52 +167,31 @@
         resp_locals.append(
             chunked_pass(resp_x[item], resp_dt[item], resp_b[item], resp_c[item], resp_rates)
         )
-    prompt_rates = lax.dynamic_slice_in_dim(ssm_rate, resp_index * prompt_heads, prompt_heads)
-    local_outs = []
-    local_states = []
-    prompt_decays = []
-    log_totals = []
+    heads_per_chain = prompt_heads // seq_count
+    chain_x = lax.all_to_all(prompt_x, "seq", split_axis=2, concat_axis=1, tiled=True)
+    chain_dt = lax.all_to_all(prompt_dt, "seq", split_axis=1, concat_axis=2, tiled=True)
+    chain_b = lax.all_gather(prompt_b, "seq", axis=1, tiled=True)
+    chain_c = lax.all_gather(prompt_c, "seq", axis=1, tiled=True)
+    chain_rates = lax.dynamic_slice_in_dim(
+        ssm_rate, resp_index * prompt_heads + seq_index * heads_per_chain, heads_per_chain
+    )
+    chain_outs = []
+    chain_finals = []
     for prompt in range(prompt_count):
-        out, final, decays_to, total = sequence_pass(
-            prompt_x[prompt], prompt_dt[prompt], prompt_b[prompt], prompt_c[prompt], prompt_rates
+        out, final, decays_to, total = chunked_pass(
+            chain_x[prompt], chain_dt[prompt], chain_b[prompt], chain_c[prompt], chain_rates
         )
-        local_outs.append(out)
-        local_states.append(final)
-        prompt_decays.append(decays_to)
-        log_totals.append(total)
-    local_state = jnp.stack(local_states)
-    decay_total = jnp.exp(jnp.stack(log_totals))
-    gathered_states = lax.all_gather(local_state, "seq")
-    slot = lax.broadcasted_iota(jnp.int32, (seq_count,) + decay_total.shape, 0)
-    gathered_decays = lax.psum(jnp.where(slot == seq_index, decay_total[None], 0.0), "seq")
+        chain_outs.append(head_norm(out).astype(jnp.bfloat16))
+        chain_finals.append(final)
+    prompt_ssm_out = lax.all_to_all(
+        jnp.stack(chain_outs), "seq", split_axis=1, concat_axis=2, tiled=True
+    )
+    finals = lax.all_gather(jnp.stack(chain_finals), "seq", axis=1, tiled=True)
     heads_here = resp_query.shape[2] // HDIM
     own_head = seq_index // repeat
     resp_attn_out = response_attention(
         resp_query, moved_keys, moved_values, resp_keys, resp_values, resp_group, resp_len, own_head
     )
-    gathered_states, resp_attn_out = lax.optimization_barrier((gathered_states, resp_attn_out))
-    shard = lax.broadcasted_iota(jnp.int32, (seq_count, seq_count), 0)
-    later = lax.broadcasted_iota(jnp.int32, (seq_count, seq_count), 1)
-    between = (later > shard) & (later < seq_index)
-    after = later > shard
-    factors = gathered_decays[None]
-    before_weights = jnp.prod(jnp.where(between[:, :, None, None], factors, 1.0), axis=1)
-    before_weights = jnp.where((shard[:, 0] < seq_index)[:, None, None], before_weights, 0.0)
-    final_weights = jnp.prod(jnp.where(after[:, :, None, None], factors, 1.0), axis=1)
-    arriving_state = jnp.sum(before_weights[:, :, :, None, None] * gathered_states, axis=0)
-    inclusive = jnp.sum(final_weights[:, :, :, None, None] * gathered_states, axis=0)
-    prompt_outs = []
-    for prompt in range(prompt_count):
-        carried = jnp.einsum(
-            "tn,hdn->thd",
-            prompt_c[prompt].astype(jnp.float32),
-            arriving_state[prompt],
-            precision=lax.Precision.HIGHEST,
-        )
-        corrected = local_outs[prompt] + jnp.exp(prompt_decays[prompt]).T[:, :, None] * carried
-        prompt_outs.append(head_norm(corrected).astype(jnp.bfloat16))
-    prompt_ssm_out = jnp.stack(prompt_outs)
-    finals = inclusive
     ratio = seq_count // lax.axis_size("resp")
     piece = lax.dynamic_slice_in_dim(finals, seq_index % ratio * resp_heads, resp_heads, 1)
     start_states = broadcast(piece, "resp", seq_index // ratio)

time: 397 us -> 338 us (0.85)
  blocking collectives: 62.2 us -> 0 us
  waiting for transfers between devices: 94.5 us -> 42.8 us
  starting transfers between devices: 11.6 us -> 31.5 us
  local copies, waits for them, and re-layouts: 64.7 us -> 84.3 us
  Pallas kernels: 56.7 us -> 76.1 us
  matrix products: 37.1 us -> 32.4 us
    psum x1, waiting for transfers between devices: 86.1 us -> 0.01 us  [broadcast(): return lax.psum(kept, axis)]
    psum x1 -> x0, blocking collectives: 62.2 us -> none  [body(): lax.psum(jnp.where(slot == seq_index, decay_total[None], 0.0), 'seq')]
    all_gather x1 -> x3, waiting for transfers between devices: 0.01 us -> 25 us  [the longest x1 25 us: body(): finals = lax.all_gather(jnp.stack(chain_finals), 'seq', axis=1, tiled=True)]
    all_to_all x0 -> x3, starting transfers between devices: none -> 20.4 us  [the longest x1 7.04 us: body(): lax.all_to_all(prompt_x, 'seq', split_axis=2, concat_axis=1, tiled=True)]
    pallas_call x1, Pallas kernels: 56.7 us -> 76.1 us  [response_attention(): pl.pallas_call(kernel, grid_spec=grid_spec, out_shape=jax.ShapeDtypeStruc...]
    unnamed x12 -> x40, other arithmetic: 1.76 us -> 21.1 us
    reduce_sum x1 -> x0, other arithmetic: 13.9 us -> none  [body(): jnp.sum(before_weights[:, :, :, None, None] * gathered_states, axis=0)]
    all_to_all x0 -> x3, waiting for transfers between devices: none -> 11 us  [the longest x1 11 us: body(): lax.all_to_all(prompt_x, 'seq', split_axis=2, concat_axis=1, tiled=True)]
  transfers between devices with their start and end apart: 4 -> 9, of which waited for: 2 -> 3; matrix products, arithmetic and copies ran while one was open for 26% -> 42% of each run, Pallas kernels for 14% -> 23%
where the time goes in v2:
time: 338 us; the launch traced here: 332 us
  local copies, waits for them, and re-layouts  84.3 us (25%)
  Pallas kernels  76.1 us (23%)
  other arithmetic  45.9 us (14%)
  waiting for transfers between devices  42.8 us (13%)
  matrix products  32.4 us (10%)
  starting transfers between devices  31.5 us (9%)
  between operations  18.9 us (6%)
    pallas_call x1, Pallas kernels, response_attention(): pl.pallas_call(kernel, grid_spec=grid_spec, out_shape=jax.ShapeDtypeStruc...  76.1 us
    all_gather x1, waiting for transfers between devices, body(): finals = lax.all_gather(jnp.stack(chain_finals), 'seq', axis=1, tiled=True)  25 us
    another operation x4, local copies, waits for them, and re-layouts, chunked_pass(): xs = inputs.reshape(blocks, QS, heads, SP).transpose(0, 2, 1, 3)  21.3 us
    unnamed x40, other arithmetic  21.1 us
    dot_general x4, matrix products, chunked_pass(): jnp.einsum('ctn,chpn->chtp', cs.astype(jnp.float32), before, precision=la...  11.6 us
    all_to_all x1, waiting for transfers between devices, body(): lax.all_to_all(prompt_x, 'seq', split_axis=2, concat_axis=1, tiled=True)  11 us
    unnamed x90, local copies, waits for them, and re-layouts  10.8 us
    dot_general x2, matrix products, body(): jnp.einsum('tn,hdn->thd', resp_c[item].astype(jnp.float32), initial, prec...  9.27 us
  transfers between devices with their start and end apart: 9, of which 3 were waited for; matrix products, arithmetic and copies ran while one was open for 42% of the time, Pallas kernels for 23%

profile of v2, /device:TPU:33, one launch (start us, length us, event | category | flops | bytes accessed | tf_op | source)
XLA Modules:
  0.0 331.9 jit_solution(11894965962060587092)
XLA Ops:
  9.3 6.8 %all-to-all-start.2 = ((f32[2,32,128]{2,0,1:T(2,128)}), f32[2,32,128]{2,0,1:T(2,128)}, u32[]{:S(2)}, u32[]{:S(2)}) async-start(f32[2,32,128]{2,0,1:T(2,128)} %copy.107), calls=%async_computation.2 | async-start | bytes 65536 | tf_op jit(solution)/shard_map/all_to_all | solution.py:172
  30.9 4.0 %fusion.70 = (bf16[1,1024,1024]{2,1,0:T(8,128)(2,1)S(1)}, bf16[1,1024,1024]{2,1,0:T(8,128)(2,1)}) fusion(bf16[2,1024,1024]{2,1,0:T(8,128)(2,1)} %param.25), kind=kLoop, calls=%fused_computation.299 | loop fusion | bytes 8388608 | tf_op jit(solution)/shard_map/slice | solution.py:168
  34.9 3.9 %reshape.661 = bf16[8,128,16,64]{3,2,1,0:T(8,128)(2,1)} reshape(bf16[1,1024,1024]{2,1,0:T(8,128)(2,1)S(1)} %get-tuple-element.107) | data formatting | bytes 4194304 | tf_op jit(solution)/shard_map/reshape;squeeze | solution.py:76
  38.8 5.1 %copy.104 = bf16[8,128,16,64]{1,3,2,0:T(8,128)(2,1)S(1)} copy(bf16[8,128,16,64]{3,2,1,0:T(8,128)(2,1)} %reshape.661) | data formatting | bytes 4194304 | tf_op jit(solution)/shard_map/reshape;squeeze | solution.py:76
  49.2 6.3 %reshape.662 = bf16[8,128,16,64]{3,2,1,0:T(8,128)(2,1)} reshape(bf16[1,1024,1024]{2,1,0:T(8,128)(2,1)} %get-tuple-element.108) | data formatting | bytes 4194304 | tf_op jit(solution)/shard_map/reshape;squeeze | solution.py:76
  55.5 5.9 %copy.117 = bf16[8,128,16,64]{1,3,2,0:T(8,128)(2,1)} copy(bf16[8,128,16,64]{3,2,1,0:T(8,128)(2,1)} %reshape.662) | data formatting | bytes 4194304 | tf_op jit(solution)/shard_map/reshape;squeeze | solution.py:76
  68.4 3.0 fusion
  71.5 3.0 fusion.1
  74.8 3.9 %fusion.5 = f32[8,16,8,8,128]{4,3,2,1,0:T(8,128)} fusion(f32[8,16,128,64]{2,3,1,0:T(8,128)S(1)} %fusion, f32[8,16,64,128]{3,2,1,0:T(8,128)S(1)} %fusion.47, bf16[8,128,128,1]{2,1,3,0:T(8,128)(2,1)S(1)} %bitcast.367, f32[8,128,16]{1,2,0:T(8,128)S(1)} %get-tuple-element.125), kind=kOutput, calls=%fused_computation.14 | convolution fusion | flops 1612709888 | bytes 12910592 | tf_op jit(solution)/shard_map/ctn,chpn->chtp/dot_general | solution.py:106
  78.8 3.9 %fusion.3 = f32[8,16,8,8,128]{4,3,2,1,0:T(8,128)} fusion(f32[8,16,128,64]{2,3,1,0:T(8,128)S(1)} %fusion.1, f32[8,16,64,128]{3,2,1,0:T(8,128)S(1)} %fusion.46, bf16[8,128,128,1]{2,1,3,0:T(8,128)(2,1)S(1)} %bitcast.365, f32[8,128,16]{1,2,0:T(8,128)S(1)} %get-tuple-element.127), kind=kOutput, calls=%fused_computation.10 | convolution fusion | flops 1612709888 | bytes 12910592 | tf_op jit(solution)/shard_map/ctn,chpn->chtp/dot_general | solution.py:106
  90.3 4.3 %reshape.641.q_ref = bf16[2,4096,128]{2,1,0:T(8,128)(2,1)} reshape(bf16[2,1024,512]{2,1,0:T(8,128)(2,1)} %param.18) | data formatting | bytes 4194304 | tf_op jit(solution)/shard_map/reshape | solution.py:222
  96.0 7.0 %all-to-all-start.3 = ((bf16[2,128,2048]{1,0,2:T(2,128)(2,1)}), bf16[2,128,2048]{1,0,2:T(2,128)(2,1)S(1)}, u32[]{:S(2)}, u32[]{:S(2)}) async-start(bf16[2,128,2048]{1,0,2:T(2,128)(2,1)} %copy.110), calls=%async_computation.3 | async-start | bytes 2097152 | tf_op jit(solution)/shard_map/all_to_all | solution.py:171
  107.3 11.0 %all-to-all-done.3 = bf16[2,128,2048]{1,0,2:T(2,128)(2,1)S(1)} async-done(((bf16[2,128,2048]{1,0,2:T(2,128)(2,1)}), bf16[2,128,2048]{1,0,2:T(2,128)(2,1)S(1)}, u32[]{:S(2)}, u32[]{:S(2)}) %all-to-all-start.3) | async-done | bytes 1048608 | tf_op jit(solution)/shard_map/all_to_all | solution.py:171
  120.0 4.3 %all-to-all-start.1 = ((bf16[2,128,2048]{1,0,2:T(2,128)(2,1)}), bf16[2,128,2048]{1,0,2:T(2,128)(2,1)}, u32[]{:S(2)}, u32[]{:S(2)}) async-start(bf16[2,128,2048]{1,0,2:T(2,128)(2,1)} %bitcast.7), calls=%async_computation.1 | async-start | bytes 2097152 | tf_op jit(solution)/shard_map/all_to_all | solution.py:162
  147.1 2.8 broadcast_in_dim.58
  149.9 6.6 %all-to-all-start = ((bf16[2,128,2048]{1,0,2:T(2,128)(2,1)}), bf16[2,128,2048]{1,0,2:T(2,128)(2,1)}, u32[]{:S(2)}, u32[]{:S(2)}) async-start(bf16[2,128,2048]{1,0,2:T(2,128)(2,1)} %bitcast.358), calls=%async_computation | async-start | bytes 2097152 | tf_op jit(solution)/shard_map/all_to_all | solution.py:161
  163.4 5.4 %all-to-all-done = bf16[2,128,2048]{1,0,2:T(2,128)(2,1)} async-done(((bf16[2,128,2048]{1,0,2:T(2,128)(2,1)}), bf16[2,128,2048]{1,0,2:T(2,128)(2,1)}, u32[]{:S(2)}, u32[]{:S(2)}) %all-to-all-start) | async-done | bytes 1048608 | tf_op jit(solution)/shard_map/all_to_all | solution.py:161
  187.8 6.6 %all-to-all-start.4 = ((bf16[2,2048,128]{2,0,1:T(2,128)(2,1)}), bf16[2,2048,128]{2,0,1:T(2,128)(2,1)S(1)}, u32[]{:S(2)}, u32[]{:S(2)}) async-start(bf16[2,2048,128]{2,0,1:T(2,128)(2,1)} %copy.131), calls=%async_computation.4 | async-start | bytes 2097152 | tf_op jit(solution)/shard_map/all_to_all | solution.py:186
  194.4 25.0 %all-gather.6.cloned.1.call-done = f32[2,32,64,128]{3,2,1,0:T(8,128)} async-done(((f32[2,2,64,128]{3,2,1,0:T(8,128)}), f32[2,32,64,128]{3,2,1,0:T(8,128)}) %all-gather.6.cloned.1.call-update) | async-done | bytes 2097168 | tf_op jit(solution)/shard_map/all_gather | solution.py:189
  221.8 76.1 %shard_map.175 = bf16[2,4096,128]{2,1,0:T(8,128)(2,1)} custom-call(s32[2]{0:T(128)} %group_ref.1, s32[2]{0:T(128)} %len_ref.1, s32[1]{0:T(128)} %bitcast.head_ref, bf16[2,4096,128]{2,1,0:T(8,128)(2,1)} %reshape.641.q_ref, bf16[2,2048,128]{2,1,0:T(8,128)(2,1)} %bitcast.379, bf16[2,2048,128]{2,1,0:T(8,128)(2,1)} %bitcast.378, bf16[2,1024,1024]{2,1,0:T(8,128)(2,1)} %rk_ref.1, ...), custom_call_target="tpu_custom_call" | custom-call | flops 12884901888 | bytes 7340032 | tf_op jit(solution)/shard_map/pallas_call | solution.py:276
  297.9 4.3 %reshape.644 = bf16[2,1024,512]{2,1,0:T(8,128)(2,1)} reshape(bf16[2,4096,128]{2,1,0:T(8,128)(2,1)} %shard_map.175) | data formatting | bytes 4194304 | tf_op jit(solution)/shard_map/reshape | solution.py:284
  304.4 4.6 %multiply_reduce_fusion.1 = (f32[1024,16]{0,1:T(8,128)S(1)}, f32[1024,16,64]{0,2,1:T(8,128)S(1)}) fusion(bf16[2,1024,128]{2,1,0:T(8,128)(2,1)S(1)} %copy-done.4, f32[2,16,64,128]{3,2,1,0:T(8,128)} %all-reduce.2.cloned.1.call-done, s32[]{:T(128)S(6)} %select_n.79, f32[1024,16]{0,1:T(8,128)S(1)} %bitcast_bitcast_fusion.1, f32[8,16,8,8,128]{4,3,2,1,0:T(8,128)} %fusion.5), kind=kOutput, calls=%fused_computation.23 | convolution fusion | flops 1614790656 | bytes 9306116 | tf_op jit(solution)/shard_map/tn,hdn->thd/dot_general | solution.py:203
  309.7 2.6 copy.114
  312.3 4.6 %multiply_reduce_fusion = (f32[1024,16]{0,1:T(8,128)S(1)}, f32[1024,16,64]{0,2,1:T(8,128)S(1)}) fusion(bf16[2,1024,128]{2,1,0:T(8,128)(2,1)S(1)} %copy-done.4, f32[2,16,64,128]{3,2,1,0:T(8,128)} %all-reduce.2.cloned.1.call-done, s32[]{:T(128)S(6)} %select_n.82, f32[1024,16]{0,1:T(8,128)S(1)} %bitcast_bitcast_fusion, f32[8,16,8,8,128]{4,3,2,1,0:T(8,128)} %fusion.3), kind=kOutput, calls=%fused_computation.16 | convolution fusion | flops 1614790656 | bytes 9306116 | tf_op jit(solution)/shard_map/tn,hdn->thd/dot_general | solution.py:203
  (243 shorter events, 101.7 us)
Async XLA Ops:
  7.2 118.4 %all-gather.4.cloned.1.call-start = ((), (), s32[]{:S(2)}) async-start(), calls=%async_computation.5 | async-start | bytes 1114112 | tf_op jit(solution)/shard_map/all_gather | solution.py:173
  9.3 86.7 %all-to-all-start.2 = ((f32[2,32,128]{2,0,1:T(2,128)}), f32[2,32,128]{2,0,1:T(2,128)}, u32[]{:S(2)}, u32[]{:S(2)}) async-start(f32[2,32,128]{2,0,1:T(2,128)} %copy.107), calls=%async_computation.2 | async-start | bytes 65536 | tf_op jit(solution)/shard_map/all_to_all | solution.py:172
  16.1 155.3 %all-gather.8.cloned.1.call-start = ((), (), s32[]{:S(2)}) async-start(), calls=%async_computation.8 | async-start | bytes 1114112 | tf_op jit(solution)/shard_map/all_gather | solution.py:174
  38.8 5.1 %copy-start.11 = (bf16[2,1024,128]{2,1,0:T(8,128)(2,1)S(1)}, bf16[2,1024,128]{2,1,0:T(8,128)(2,1)}, u32[]{:S(2)}) copy-start(bf16[2,1024,128]{2,1,0:T(8,128)(2,1)} %param.27) | copy-start | bytes 1572868
  78.7 4.1 %copy-start.19 = (f32[16]{0:T(128)S(1)}, f32[16]{0:T(128)}, u32[]{:S(2)}) copy-start(f32[16]{0:T(128)} %get-tuple-element.22) | copy-start | bytes 196
  78.7 4.1 %copy-start.31 = (f32[16]{0:T(128)S(1)}, f32[16]{0:T(128)}, u32[]{:S(2)}) copy-start(f32[16]{0:T(128)} %get-tuple-element.16) | copy-start | bytes 196
  78.7 4.1 %copy-start.32 = (f32[16]{0:T(128)S(1)}, f32[16]{0:T(128)}, u32[]{:S(2)}) copy-start(f32[16]{0:T(128)} %get-tuple-element.17) | copy-start | bytes 196
  78.8 4.1 %copy-start.33 = (f32[16]{0:T(128)S(1)}, f32[16]{0:T(128)}, u32[]{:S(2)}) copy-start(f32[16]{0:T(128)} %get-tuple-element.18) | copy-start | bytes 196
  78.8 4.1 %copy-start.34 = (f32[16]{0:T(128)S(1)}, f32[16]{0:T(128)}, u32[]{:S(2)}) copy-start(f32[16]{0:T(128)} %get-tuple-element.19) | copy-start | bytes 196
  78.8 7.9 %copy-start.39 = (f32[256]{0:T(256)S(1)}, f32[256]{0:T(256)}, u32[]{:S(2)}) copy-start(f32[256]{0:T(256)} %param.29) | copy-start | bytes 3076
  78.8 8.0 %copy-start.10 = (bf16[2,128,2048]{2,1,0:T(8,128)(2,1)S(1)}, bf16[2,128,2048]{2,1,0:T(8,128)(2,1)}, u32[]{:S(2)}) copy-start(bf16[2,128,2048]{2,1,0:T(8,128)(2,1)} %param.21) | copy-start | bytes 3145732
  78.8 10.0 %copy-start.12 = (bf16[2,128,1024]{2,1,0:T(8,128)(2,1)S(1)}, bf16[2,128,1024]{2,1,0:T(8,128)(2,1)}, u32[]{:S(2)}) copy-start(bf16[2,128,1024]{2,1,0:T(8,128)(2,1)} %param.17) | copy-start | bytes 1572868
  78.8 10.4 %copy-start.13 = (bf16[2,128,1024]{2,1,0:T(8,128)(2,1)S(1)}, bf16[2,128,1024]{2,1,0:T(8,128)(2,1)}, u32[]{:S(2)}) copy-start(bf16[2,128,1024]{2,1,0:T(8,128)(2,1)} %param.16) | copy-start | bytes 1572868
  96.0 22.3 %all-to-all-start.3 = ((bf16[2,128,2048]{1,0,2:T(2,128)(2,1)}), bf16[2,128,2048]{1,0,2:T(2,128)(2,1)S(1)}, u32[]{:S(2)}, u32[]{:S(2)}) async-start(bf16[2,128,2048]{1,0,2:T(2,128)(2,1)} %copy.110), calls=%async_computation.3 | async-start | bytes 2097152 | tf_op jit(solution)/shard_map/all_to_all | solution.py:171
  120.0 27.1 %all-to-all-start.1 = ((bf16[2,128,2048]{1,0,2:T(2,128)(2,1)}), bf16[2,128,2048]{1,0,2:T(2,128)(2,1)}, u32[]{:S(2)}, u32[]{:S(2)}) async-start(bf16[2,128,2048]{1,0,2:T(2,128)(2,1)} %bitcast.7), calls=%async_computation.1 | async-start | bytes 2097152 | tf_op jit(solution)/shard_map/all_to_all | solution.py:162
  125.6 10.1 %copy-start.7 = (bf16[1,16,128,128]{2,3,1,0:T(8,128)(2,1)}, bf16[1,16,128,128]{2,3,1,0:T(8,128)(2,1)S(1)}, u32[]{:S(2)}) copy-start(bf16[1,16,128,128]{2,3,1,0:T(8,128)(2,1)S(1)} %get-tuple-element.115) | copy-start | bytes 1572868
  125.6 10.1 %copy-start.5 = (bf16[1,16,128,128]{2,3,1,0:T(8,128)(2,1)S(1)}, bf16[1,16,128,128]{2,3,1,0:T(8,128)(2,1)}, u32[]{:S(2)}) copy-start(bf16[1,16,128,128]{2,3,1,0:T(8,128)(2,1)} %get-tuple-element.116) | copy-start | bytes 1572868
  129.4 17.0 %copy-start.24 = (f32[2]{0:T(128)S(1)}, f32[2]{0:T(128)}, u32[]{:S(2)}) copy-start(f32[2]{0:T(128)} %get-tuple-element.53) | copy-start | bytes 28
  149.9 18.8 %all-to-all-start = ((bf16[2,128,2048]{1,0,2:T(2,128)(2,1)}), bf16[2,128,2048]{1,0,2:T(2,128)(2,1)}, u32[]{:S(2)}, u32[]{:S(2)}) async-start(bf16[2,128,2048]{1,0,2:T(2,128)(2,1)} %bitcast.358), calls=%async_computation | async-start | bytes 2097152 | tf_op jit(solution)/shard_map/all_to_all | solution.py:161
  156.5 62.9 %all-gather.6.cloned.1.call-start = ((), (), s32[]{:S(2)}) async-start(), calls=%async_computation.6 | async-start | bytes 2228224 | tf_op jit(solution)/shard_map/all_gather | solution.py:189
  163.4 9.9 %copy-start.8 = (bf16[1,16,128,128]{2,3,1,0:T(8,128)(2,1)S(1)}, bf16[1,16,128,128]{2,3,1,0:T(8,128)(2,1)}, u32[]{:S(2)}) copy-start(bf16[1,16,128,128]{2,3,1,0:T(8,128)(2,1)} %copy-done.7) | copy-start | bytes 1572868
  174.2 4.8 %copy-start.6 = (bf16[1,16,128,128]{2,3,1,0:T(8,128)(2,1)S(1)}, bf16[1,16,128,128]{2,3,1,0:T(8,128)(2,1)}, u32[]{:S(2)}) copy-start(bf16[1,16,128,128]{2,3,1,0:T(8,128)(2,1)} %get-tuple-element.116) | copy-start | bytes 1572868
  187.8 114.5 %all-to-all-start.4 = ((bf16[2,2048,128]{2,0,1:T(2,128)(2,1)}), bf16[2,2048,128]{2,0,1:T(2,128)(2,1)S(1)}, u32[]{:S(2)}, u32[]{:S(2)}) async-start(bf16[2,2048,128]{2,0,1:T(2,128)(2,1)} %copy.131), calls=%async_computation.4 | async-start | bytes 2097152 | tf_op jit(solution)/shard_map/all_to_all | solution.py:186
  194.4 110.1 %all-reduce.2.cloned.1.call-start = ((), (), s32[]{:S(2)}) async-start(), calls=%async_computation.7 | async-start | bytes 2097152 | tf_op jit(solution)/shard_map/psum | solution.py:27
  (25 other events, 70.2 us)
Sparse Core Ops, SparseCore 0:
  10.2 43.2 all-gather.3
  55.7 41.8 all-gather.7
  160.0 59.3 all-gather.5
  221.9 57.8 all-reduce.1

commit v3 on v2

--- a/solution.py
+++ b/solution.py
@@ -172,6 +172,7 @@
     chain_dt = lax.all_to_all(prompt_dt, "seq", split_axis=1, concat_axis=2, tiled=True)
     chain_b = lax.all_gather(prompt_b, "seq", axis=1, tiled=True)
     chain_c = lax.all_gather(prompt_c, "seq", axis=1, tiled=True)
+    chain_x, chain_dt, resp_locals = lax.optimization_barrier((chain_x, chain_dt, resp_locals))
     chain_rates = lax.dynamic_slice_in_dim(
         ssm_rate, resp_index * prompt_heads + seq_index * heads_per_chain, heads_per_chain
     )
@@ -186,15 +187,20 @@
     prompt_ssm_out = lax.all_to_all(
         jnp.stack(chain_outs), "seq", split_axis=1, concat_axis=2, tiled=True
     )
-    finals = lax.all_gather(jnp.stack(chain_finals), "seq", axis=1, tiled=True)
-    heads_here = resp_query.shape[2] // HDIM
+    chain_final, resp_query = lax.optimization_barrier((jnp.stack(chain_finals), resp_query))
+    finals = lax.all_gather(chain_final, "seq", axis=1, tiled=True)
     own_head = seq_index // repeat
-    resp_attn_out = response_attention(
-        resp_query, moved_keys, moved_values, resp_keys, resp_values, resp_group, resp_len, own_head
-    )
+    attention_args = (moved_keys, moved_values, resp_keys, resp_values, resp_group, resp_len, own_head)
+    first_out = response_attention(resp_query, *attention_args, 0)
     ratio = seq_count // lax.axis_size("resp")
     piece = lax.dynamic_slice_in_dim(finals, seq_index % ratio * resp_heads, resp_heads, 1)
+    piece, first_out, resp_query = lax.optimization_barrier((piece, first_out, resp_query))
     start_states = broadcast(piece, "resp", seq_index // ratio)
+    outs = [first_out]
+    for item in range(1, responses_here):
+        outs.append(response_attention(resp_query, *attention_args, item))
+    start_states, outs = lax.optimization_barrier((start_states, outs))
+    resp_attn_out = jnp.concatenate(outs, axis=0)
     positions = lax.broadcasted_iota(jnp.int32, (slots,), 0)
     resp_outs = []
     for item in range(responses_here):
@@ -215,11 +221,12 @@
 
 ROWS = 512
 
-def response_attention(resp_query, prompt_keys, prompt_values, resp_keys, resp_values, group, length, head):
-    items, slots, width = resp_query.shape
+def response_attention(resp_query, prompt_keys, prompt_values, resp_keys, resp_values, group, length, head, which):
+    _, slots, width = resp_query.shape
+    items = 1
     heads = width // HDIM
     rows = slots * heads
-    queries = resp_query.reshape(items, rows, HDIM)
+    queries = resp_query.reshape(resp_query.shape[0], rows, HDIM)
     prompt_len = prompt_keys.shape[1]
     tile = min(ROWS, rows)
     scale = 1.0 / math.sqrt(HDIM)
@@ -227,7 +234,7 @@
     def kernel(group_ref, len_ref, head_ref, q_ref, pk_ref, pv_ref, rk_ref, rv_ref, o_ref):
         item = pl.program_id(0)
         block = pl.program_id(1)
-        window_extent = len_ref[item]
+        window_extent = len_ref[which + item]
         first = block * (tile // heads)
 
         @pl.when(first >= window_extent)
@@ -265,11 +272,11 @@
         num_scalar_prefetch=3,
         grid=(items, rows // tile),
         in_specs=[
-            pl.BlockSpec((1, tile, HDIM), lambda i, b, g, n, h: (i, b, 0)),
-            pl.BlockSpec((1, prompt_len, HDIM), lambda i, b, g, n, h: (g[i], 0, 0)),
-            pl.BlockSpec((1, prompt_len, HDIM), lambda i, b, g, n, h: (g[i], 0, 0)),
-            pl.BlockSpec((1, slots, HDIM), lambda i, b, g, n, h: (i, 0, h[0])),
-            pl.BlockSpec((1, slots, HDIM), lambda i, b, g, n, h: (i, 0, h[0])),
+            pl.BlockSpec((1, tile, HDIM), lambda i, b, g, n, h: (which + i, b, 0)),
+            pl.BlockSpec((1, prompt_len, HDIM), lambda i, b, g, n, h: (g[which + i], 0, 0)),
+            pl.BlockSpec((1, prompt_len, HDIM), lambda i, b, g, n, h: (g[which + i], 0, 0)),
+            pl.BlockSpec((1, slots, HDIM), lambda i, b, g, n, h: (which + i, 0, h[0])),
+            pl.BlockSpec((1, slots, HDIM), lambda i, b, g, n, h: (which + i, 0, h[0])),
         ],
         out_specs=pl.BlockSpec((1, tile, HDIM), lambda i, b, g, n, h: (i, b, 0)),
     )

time: 338 us -> 351 us (1.038)
  the two profiles are of different devices: /device:TPU:33 before, /device:TPU:0 now
where the time goes in v3:
time: 351 us; the launch traced here: 345 us
  local copies, waits for them, and re-layouts  110 us (31%)
  Pallas kernels  78.1 us (22%)
  waiting for transfers between devices  38.3 us (11%)
  matrix products  37.5 us (11%)
  other arithmetic  35.9 us (10%)
  starting transfers between devices  26.2 us (7%)
  between operations  18.6 us (5%)
    pallas_call x2, Pallas kernels, response_attention(): pl.pallas_call(kernel, grid_spec=grid_spec, out_shape=jax.ShapeDtypeStruc...  78.1 us
    another operation x8, local copies, waits for them, and re-layouts, chunked_pass(): xs = inputs.reshape(blocks, QS, heads, SP).transpose(0, 2, 1, 3)  29.5 us
    psum x1, waiting for transfers between devices, broadcast(): return lax.psum(kept, axis)  21.6 us
    unnamed x105, local copies, waits for them, and re-layouts  13.1 us
    dot_general x4, matrix products, chunked_pass(): jnp.einsum('ctn,chpn->chtp', cs.astype(jnp.float32), before, precision=la...  12.6 us
    unnamed x40, other arithmetic  12.6 us
    reshape x1, local copies, waits for them, and re-layouts, body(): prompt_keys.reshape(prompt_count, shard_rows, memory_head_number, HDIM)  12.6 us
    dot_general x4, matrix products, chunked_pass(): jnp.einsum('chtu,chup->chtp', mixing, xs, preferred_element_type=jnp.floa...  12 us
  transfers between devices with their start and end apart: 9, of which 4 were waited for; matrix products, arithmetic and copies ran while one was open for 44% of the time, Pallas kernels for 23%

profile of v3, /device:TPU:0, one launch (start us, length us, event | category | flops | bytes accessed | tf_op | source)
XLA Modules:
  0.0 345.0 jit_solution(17984991200791569657)
XLA Ops:
  9.3 7.2 %all-to-all-start.1 = ((f32[2,32,128]{2,0,1:T(2,128)}), f32[2,32,128]{2,0,1:T(2,128)}, u32[]{:S(2)}, u32[]{:S(2)}) async-start(f32[2,32,128]{2,0,1:T(2,128)} %copy.104), calls=%async_computation.1 | async-start | bytes 65536 | tf_op jit(solution)/shard_map/all_to_all | solution.py:172
  31.3 4.0 %fusion.74 = (bf16[1,1024,1024]{2,1,0:T(8,128)(2,1)}, bf16[1,1024,1024]{2,1,0:T(8,128)(2,1)S(1)}) fusion(bf16[2,1024,1024]{2,1,0:T(8,128)(2,1)} %param.25), kind=kLoop, calls=%fused_computation.307 | loop fusion | bytes 8388608 | tf_op jit(solution)/shard_map/slice | solution.py:168
  35.3 3.9 %reshape.670 = bf16[8,128,16,64]{3,2,1,0:T(8,128)(2,1)} reshape(bf16[1,1024,1024]{2,1,0:T(8,128)(2,1)S(1)} %get-tuple-element.136) | data formatting | bytes 4194304 | tf_op jit(solution)/shard_map/reshape;squeeze | solution.py:76
  39.2 5.0 %copy.108 = bf16[8,128,16,64]{1,3,2,0:T(8,128)(2,1)S(1)} copy(bf16[8,128,16,64]{3,2,1,0:T(8,128)(2,1)} %reshape.670) | data formatting | bytes 4194304 | tf_op jit(solution)/shard_map/reshape;squeeze | solution.py:76
  46.8 6.4 %reshape.671 = bf16[8,128,16,64]{3,2,1,0:T(8,128)(2,1)} reshape(bf16[1,1024,1024]{2,1,0:T(8,128)(2,1)} %get-tuple-element.135) | data formatting | bytes 4194304 | tf_op jit(solution)/shard_map/reshape;squeeze | solution.py:76
  53.2 5.8 %copy.113 = bf16[8,128,16,64]{1,3,2,0:T(8,128)(2,1)} copy(bf16[8,128,16,64]{3,2,1,0:T(8,128)(2,1)} %reshape.671) | data formatting | bytes 4194304 | tf_op jit(solution)/shard_map/reshape;squeeze | solution.py:76
  68.3 3.1 fusion
  71.4 6.0 %fusion.1 = f32[8,16,128,64]{2,3,1,0:T(8,128)} fusion(f32[8,16,128]{2,1,0:T(8,128)S(1)} %bitcast.405, f32[8,128,128]{2,1,0:T(8,128)S(1)} %fusion.83, f32[8,16,128]{2,1,0:T(8,128)S(1)} %reduce_window_sum.40, pred[128,128]{1,0:T(8,128)(4,1)S(1)} %iota_compare_fusion, bf16[8,128,16,64]{1,3,2,0:T(8,128)(2,1)S(1)} %copy-done.1), kind=kOutput, calls=%fused_computation.3 | convolution fusion | flops 278921216 | bytes 6963200 | tf_op jit(solution)/shard_map/chtu,chup->chtp/dot_general | solution.py:89
  79.6 4.0 %fusion.7 = f32[8,16,8,8,128]{4,3,2,1,0:T(8,128)} fusion(f32[8,16,128,64]{2,3,1,0:T(8,128)S(1)} %fusion, f32[8,16,64,128]{3,2,1,0:T(8,128)S(1)} %fusion.49, bf16[8,128,128,1]{2,1,3,0:T(8,128)(2,1)S(1)} %bitcast.387, f32[8,128,16]{1,2,0:T(8,128)S(1)} %get-tuple-element.155), kind=kOutput, calls=%fused_computation.16 | convolution fusion | flops 1612709888 | bytes 12910592 | tf_op jit(solution)/shard_map/ctn,chpn->chtp/dot_general | solution.py:106
  87.0 12.6 %copy.160 = bf16[2,128,1024]{1,0,2:T(2,128)(2,1)S(1)} copy(bf16[2,128,1024]{2,1,0:T(8,128)(2,1)S(1)} %copy-done.17) | data formatting | bytes 1048576 | tf_op jit(solution)/shard_map/reshape | solution.py:155
  99.5 7.2 %all-to-all-start = ((bf16[2,128,2048]{1,0,2:T(2,128)(2,1)}), bf16[2,128,2048]{1,0,2:T(2,128)(2,1)S(1)}, u32[]{:S(2)}, u32[]{:S(2)}) async-start(bf16[2,128,2048]{1,0,2:T(2,128)(2,1)} %copy.101), calls=%async_computation | async-start | bytes 2097152 | tf_op jit(solution)/shard_map/all_to_all | solution.py:171
  106.7 6.1 %fusion.5 = f32[8,16,8,8,128]{4,3,2,1,0:T(8,128)S(1)} fusion(f32[8,16,128,64]{2,3,1,0:T(8,128)} %fusion.1, f32[8,16,64,128]{3,2,1,0:T(8,128)} %copy-done.5, bf16[8,128,128,1]{2,1,3,0:T(8,128)(2,1)S(1)} %bitcast.385, f32[8,128,16]{1,2,0:T(8,128)S(1)} %get-tuple-element.153), kind=kOutput, calls=%fused_computation.13 | convolution fusion | flops 1612709888 | bytes 12910592 | tf_op jit(solution)/shard_map/ctn,chpn->chtp/dot_general | solution.py:106
  112.9 4.5 %copy_bitcast_fusion = (f32[1024,16,64]{0,2,1:T(8,128)}, f32[1024,16,64]{0,2,1:T(8,128)}) fusion(f32[8,16,8,8,128]{4,3,2,1,0:T(8,128)S(1)} %fusion.5, f32[8,16,8,8,128]{4,3,2,1,0:T(8,128)S(1)} %copy-done), kind=kLoop, calls=%fused_computation.4 | loop fusion | bytes 16777216 | tf_op jit(solution)/shard_map/reshape | solution.py:111
  117.4 6.2 %all-to-all-done = bf16[2,128,2048]{1,0,2:T(2,128)(2,1)S(1)} async-done(((bf16[2,128,2048]{1,0,2:T(2,128)(2,1)}), bf16[2,128,2048]{1,0,2:T(2,128)(2,1)S(1)}, u32[]{:S(2)}, u32[]{:S(2)}) %all-to-all-start) | async-done | bytes 1048608 | tf_op jit(solution)/shard_map/all_to_all | solution.py:171
  125.3 3.7 %all-to-all-start.2 = ((bf16[2,128,2048]{1,0,2:T(2,128)(2,1)}), bf16[2,128,2048]{1,0,2:T(2,128)(2,1)S(1)}, u32[]{:S(2)}, u32[]{:S(2)}) async-start(bf16[2,128,2048]{1,0,2:T(2,128)(2,1)} %bitcast.57), calls=%async_computation.2 | async-start | bytes 2097152 | tf_op jit(solution)/shard_map/all_to_all | solution.py:161
  137.8 6.4 %all-to-all-done.2 = bf16[2,128,2048]{1,0,2:T(2,128)(2,1)S(1)} async-done(((bf16[2,128,2048]{1,0,2:T(2,128)(2,1)}), bf16[2,128,2048]{1,0,2:T(2,128)(2,1)S(1)}, u32[]{:S(2)}, u32[]{:S(2)}) %all-to-all-start.2) | async-done | bytes 1048608 | tf_op jit(solution)/shard_map/all_to_all | solution.py:161
  147.1 3.7 %all-to-all-start.3 = ((bf16[2,128,2048]{1,0,2:T(2,128)(2,1)}), bf16[2,128,2048]{1,0,2:T(2,128)(2,1)S(1)}, u32[]{:S(2)}, u32[]{:S(2)}) async-start(bf16[2,128,2048]{1,0,2:T(2,128)(2,1)} %bitcast.62), calls=%async_computation.3 | async-start | bytes 2097152 | tf_op jit(solution)/shard_map/all_to_all | solution.py:162
  195.3 4.4 %all-to-all-start.4 = ((bf16[2,2048,128]{2,0,1:T(2,128)(2,1)}), bf16[2,2048,128]{2,0,1:T(2,128)(2,1)S(1)}, u32[]{:S(2)}, u32[]{:S(2)}) async-start(bf16[2,2048,128]{2,0,1:T(2,128)(2,1)} %copy.140), calls=%async_computation.4 | async-start | bytes 2097152 | tf_op jit(solution)/shard_map/all_to_all | solution.py:187
  199.8 3.0 reshape.650.q_ref
  202.8 39.0 %shard_map.175 = bf16[1,4096,128]{2,1,0:T(8,128)(2,1)} custom-call(s32[2]{0:T(128)} %group_ref.3, s32[2]{0:T(128)} %len_ref.3, s32[1]{0:T(128)} %bitcast.55.head_ref, bf16[2,4096,128]{2,1,0:T(8,128)(2,1)} %reshape.650.q_ref, bf16[2,2048,128]{2,1,0:T(8,128)(2,1)} %bitcast.394, bf16[2,2048,128]{2,1,0:T(8,128)(2,1)} %bitcast.396, ...), custom_call_target="tpu_custom_call" | custom-call | flops 6442450944 | bytes 3670016 | tf_op jit(solution)/shard_map/pallas_call | solution.py:283
  253.4 39.1 %shard_map.176 = bf16[1,4096,128]{2,1,0:T(8,128)(2,1)} custom-call(s32[2]{0:T(128)} %group_ref.3, s32[2]{0:T(128)} %len_ref.3, s32[1]{0:T(128)} %bitcast.55.head_ref, bf16[2,4096,128]{2,1,0:T(8,128)(2,1)} %reshape.654.q_ref, bf16[2,2048,128]{2,1,0:T(8,128)(2,1)} %bitcast.395, bf16[2,2048,128]{2,1,0:T(8,128)(2,1)} %bitcast.397, ...), custom_call_target="tpu_custom_call" | custom-call | flops 6442450944 | bytes 3670016 | tf_op jit(solution)/shard_map/pallas_call | solution.py:283
  294.4 21.6 %all-reduce.2.cloned.1.call-done = f32[2,16,64,128]{3,2,1,0:T(8,128)} async-done(((f32[2,16,64,128]{3,2,1,0:T(8,128)}), f32[2,16,64,128]{3,2,1,0:T(8,128)}) %all-reduce.2.cloned.1.call-update) | async-done | bytes 1048592 | tf_op jit(solution)/shard_map/psum | solution.py:27
  315.9 4.6 %multiply_reduce_fusion.1 = (f32[1024,16]{0,1:T(8,128)S(1)}, f32[1024,16,64]{0,2,1:T(8,128)S(1)}) fusion(f32[1024,16,64]{0,2,1:T(8,128)} %get-tuple-element.26, bf16[2,1024,128]{2,1,0:T(8,128)(2,1)S(1)} %copy-done.8, f32[2,16,64,128]{3,2,1,0:T(8,128)} %all-reduce.2.cloned.1.call-done, s32[]{:T(128)S(6)} %select_n.80, ...), kind=kOutput, calls=%fused_computation.20 | convolution fusion | flops 1614790656 | bytes 9306116 | tf_op jit(solution)/shard_map/tn,hdn->thd/dot_general | solution.py:209
  323.8 4.7 %multiply_reduce_fusion = (f32[1024,16]{0,1:T(8,128)S(1)}, f32[1024,16,64]{0,2,1:T(8,128)S(1)}) fusion(f32[1024,16,64]{0,2,1:T(8,128)} %get-tuple-element.29, bf16[2,1024,128]{2,1,0:T(8,128)(2,1)} %param.28, f32[2,16,64,128]{3,2,1,0:T(8,128)} %all-reduce.2.cloned.1.call-done, s32[]{:T(128)S(6)} %select_n.82, f32[1024,16]{0,1:T(8,128)S(1)} %exponential_bitcast_fusion), kind=kOutput, calls=%fused_computation.18 | convolution fusion | flops 1614790656 | bytes 9306116 | tf_op jit(solution)/shard_map/tn,hdn->thd/dot_general | solution.py:209
  (272 shorter events, 114.5 us)
Async XLA Ops:
  7.2 160.9 %all-gather.4.cloned.1.call-start = ((), (), s32[]{:S(2)}) async-start(), calls=%async_computation.5 | async-start | bytes 1114112 | tf_op jit(solution)/shard_map/all_gather | solution.py:173
  9.3 90.3 %all-to-all-start.1 = ((f32[2,32,128]{2,0,1:T(2,128)}), f32[2,32,128]{2,0,1:T(2,128)}, u32[]{:S(2)}, u32[]{:S(2)}) async-start(f32[2,32,128]{2,0,1:T(2,128)} %copy.104), calls=%async_computation.1 | async-start | bytes 65536 | tf_op jit(solution)/shard_map/all_to_all | solution.py:172
  16.5 167.0 %all-gather.8.cloned.1.call-start = ((), (), s32[]{:S(2)}) async-start(), calls=%async_computation.8 | async-start | bytes 1114112 | tf_op jit(solution)/shard_map/all_gather | solution.py:174
  39.2 5.0 %copy-start.16 = (bf16[2,1024,128]{2,1,0:T(8,128)(2,1)S(1)}, bf16[2,1024,128]{2,1,0:T(8,128)(2,1)}, u32[]{:S(2)}) copy-start(bf16[2,1024,128]{2,1,0:T(8,128)(2,1)} %param.27) | copy-start | bytes 1572868
  59.0 4.7 %copy-start.42 = (f32[16]{0:T(128)S(1)}, f32[16]{0:T(128)}, u32[]{:S(2)}) copy-start(f32[16]{0:T(128)} %get-tuple-element.175) | copy-start | bytes 196
  71.4 6.0 %copy-start.26 = (f32[16]{0:T(128)S(1)}, f32[16]{0:T(128)}, u32[]{:S(2)}) copy-start(f32[16]{0:T(128)} %get-tuple-element.170) | copy-start | bytes 196
  79.6 5.3 %copy-start.15 = (bf16[2,128,2048]{2,1,0:T(8,128)(2,1)S(1)}, bf16[2,128,2048]{2,1,0:T(8,128)(2,1)}, u32[]{:S(2)}) copy-start(bf16[2,128,2048]{2,1,0:T(8,128)(2,1)} %param.21) | copy-start | bytes 3145732
  79.6 7.3 %copy-start.17 = (bf16[2,128,1024]{2,1,0:T(8,128)(2,1)S(1)}, bf16[2,128,1024]{2,1,0:T(8,128)(2,1)}, u32[]{:S(2)}) copy-start(bf16[2,128,1024]{2,1,0:T(8,128)(2,1)} %param.16) | copy-start | bytes 1572868
  99.5 24.0 %all-to-all-start = ((bf16[2,128,2048]{1,0,2:T(2,128)(2,1)}), bf16[2,128,2048]{1,0,2:T(2,128)(2,1)S(1)}, u32[]{:S(2)}, u32[]{:S(2)}) async-start(bf16[2,128,2048]{1,0,2:T(2,128)(2,1)} %copy.101), calls=%async_computation | async-start | bytes 2097152 | tf_op jit(solution)/shard_map/all_to_all | solution.py:171
  106.7 6.1 %copy-start = (f32[8,16,8,8,128]{4,3,2,1,0:T(8,128)S(1)}, f32[8,16,8,8,128]{4,3,2,1,0:T(8,128)}, u32[]{:S(2)}) copy-start(f32[8,16,8,8,128]{4,3,2,1,0:T(8,128)} %fusion.7) | copy-start | bytes 12582916
  112.9 19.7 %copy-start.45 = (f32[256]{0:T(256)S(1)}, f32[256]{0:T(256)}, u32[]{:S(2)}) copy-start(f32[256]{0:T(256)} %param.29) | copy-start | bytes 3076
  112.9 19.8 %copy-start.18 = (bf16[2,128,1024]{2,1,0:T(8,128)(2,1)S(1)}, bf16[2,128,1024]{2,1,0:T(8,128)(2,1)}, u32[]{:S(2)}) copy-start(bf16[2,128,1024]{2,1,0:T(8,128)(2,1)} %param.17) | copy-start | bytes 1572868
  125.3 18.9 %all-to-all-start.2 = ((bf16[2,128,2048]{1,0,2:T(2,128)(2,1)}), bf16[2,128,2048]{1,0,2:T(2,128)(2,1)S(1)}, u32[]{:S(2)}, u32[]{:S(2)}) async-start(bf16[2,128,2048]{1,0,2:T(2,128)(2,1)} %bitcast.57), calls=%async_computation.2 | async-start | bytes 2097152 | tf_op jit(solution)/shard_map/all_to_all | solution.py:161
  147.1 19.6 %all-to-all-start.3 = ((bf16[2,128,2048]{1,0,2:T(2,128)(2,1)}), bf16[2,128,2048]{1,0,2:T(2,128)(2,1)S(1)}, u32[]{:S(2)}, u32[]{:S(2)}) async-start(bf16[2,128,2048]{1,0,2:T(2,128)(2,1)} %bitcast.62), calls=%async_computation.3 | async-start | bytes 2097152 | tf_op jit(solution)/shard_map/all_to_all | solution.py:162
  150.7 97.6 %all-gather.6.cloned.1.call-start = ((), (), s32[]{:S(2)}) async-start(), calls=%async_computation.6 | async-start | bytes 2228224 | tf_op jit(solution)/shard_map/all_gather | solution.py:191
  161.3 8.2 %copy-start.9 = (bf16[16,128,2,64]{1,3,2,0:T(8,128)(2,1)S(1)}, bf16[16,128,2,64]{1,3,2,0:T(8,128)(2,1)}, u32[]{:S(2)}) copy-start(bf16[16,128,2,64]{1,3,2,0:T(8,128)(2,1)} %copy.117) | copy-start | bytes 1572868
  163.9 6.6 %copy-start.29 = (f32[2]{0:T(128)S(1)}, f32[2]{0:T(128)}, u32[]{:S(2)}) copy-start(f32[2]{0:T(128)} %get-tuple-element.53) | copy-start | bytes 28
  166.8 11.3 %copy-start.10 = (bf16[16,128,2,64]{1,3,2,0:T(8,128)(2,1)S(1)}, bf16[16,128,2,64]{1,3,2,0:T(8,128)(2,1)}, u32[]{:S(2)}) copy-start(bf16[16,128,2,64]{1,3,2,0:T(8,128)(2,1)} %copy.120) | copy-start | bytes 1572868
  168.1 10.3 %copy-start.11 = (f32[16,2,64,128]{3,2,1,0:T(8,128)S(1)}, f32[16,2,64,128]{3,2,1,0:T(8,128)}, u32[]{:S(2)}) copy-start(f32[16,2,64,128]{3,2,1,0:T(8,128)} %constant_dynamic-update-slice_fusion.41) | copy-start | bytes 3145732
  193.0 6.8 %copy-start.3 = (bf16[2,1024,512]{2,1,0:T(8,128)(2,1)S(1)}, bf16[2,1024,512]{2,1,0:T(8,128)(2,1)}, u32[]{:S(2)}) copy-start(bf16[2,1024,512]{2,1,0:T(8,128)(2,1)} %param.18) | copy-start | bytes 6291460
  195.3 49.0 %all-to-all-start.4 = ((bf16[2,2048,128]{2,0,1:T(2,128)(2,1)}), bf16[2,2048,128]{2,0,1:T(2,128)(2,1)S(1)}, u32[]{:S(2)}, u32[]{:S(2)}) async-start(bf16[2,2048,128]{2,0,1:T(2,128)(2,1)} %copy.140), calls=%async_computation.4 | async-start | bytes 2097152 | tf_op jit(solution)/shard_map/all_to_all | solution.py:187
  199.7 116.2 %all-reduce.2.cloned.1.call-start = ((), (), s32[]{:S(2)}) async-start(), calls=%async_computation.7 | async-start | bytes 2097152 | tf_op jit(solution)/shard_map/psum | solution.py:27
  253.3 62.6 %copy-start.8 = (bf16[2,1024,128]{2,1,0:T(8,128)(2,1)S(1)}, bf16[2,1024,128]{2,1,0:T(8,128)(2,1)}, u32[]{:S(2)}) copy-start(bf16[2,1024,128]{2,1,0:T(8,128)(2,1)} %param.28) | copy-start | bytes 1572868
  329.2 4.7 %copy-start.44 = (pred[1024]{0:T(1024)(128)(4,1)S(1)}, pred[1024]{0:T(1024)(128)(4,1)}, u32[]{:S(2)}) copy-start(pred[1024]{0:T(1024)(128)(4,1)} %iota_compare_fusion.1) | copy-start | bytes 3076
  (31 other events, 94.4 us)
Sparse Core Ops, SparseCore 0:
  10.2 45.0 all-gather.3
  57.5 41.8 all-gather.7
  183.5 48.5 all-gather.5
  253.5 62.4 all-reduce.1

commit v4 on v2

--- a/solution.py
+++ b/solution.py
@@ -234,12 +234,13 @@
         def _():
             o_ref[...] = jnp.zeros_like(o_ref)
 
-        @pl.when(first < window_extent)
-        def _():
+        def attend(reach):
             q = q_ref[0]
             dims = (((1,), (1,)), ((), ()))
             s1 = lax.dot_general(q, pk_ref[0], dims, preferred_element_type=jnp.float32) * scale
-            s2 = lax.dot_general(q, rk_ref[0], dims, preferred_element_type=jnp.float32) * scale
+            s2 = lax.dot_general(
+                q, rk_ref[0, :reach, :], dims, preferred_element_type=jnp.float32
+            ) * scale
             position = first + lax.broadcasted_iota(jnp.int32, (tile, 1), 0) // heads
             column = lax.broadcasted_iota(jnp.int32, s2.shape, 1)
             s2 = jnp.where(column <= position, s2, -jnp.inf)
@@ -251,9 +252,21 @@
             total = jnp.sum(e1, axis=1, keepdims=True) + jnp.sum(e2, axis=1, keepdims=True)
             mixed = jnp.dot(
                 e1.astype(jnp.bfloat16), pv_ref[0], preferred_element_type=jnp.float32
-            ) + jnp.dot(e2.astype(jnp.bfloat16), rv_ref[0], preferred_element_type=jnp.float32)
+            ) + jnp.dot(
+                e2.astype(jnp.bfloat16), rv_ref[0, :reach, :], preferred_element_type=jnp.float32
+            )
             mixed = mixed / total
             o_ref[0] = jnp.where(position < window_extent, mixed, 0.0).astype(o_ref.dtype)
+
+        near = (block + 1) * (tile // heads) <= slots // 2
+
+        @pl.when((first < window_extent) & near)
+        def _():
+            attend(slots // 2)
+
+        @pl.when((first < window_extent) & jnp.logical_not(near))
+        def _():
+            attend(slots)
 
     keys_total = prompt_len + slots
     cost = pl.CostEstimate(

time: 338 us -> 328 us (0.970)
  the two profiles are of different devices: /device:TPU:33 before, /device:TPU:65 now
where the time goes in v4:
time: 328 us; the launch traced here: 322 us
  local copies, waits for them, and re-layouts  84.4 us (26%)
  Pallas kernels  65.7 us (20%)
  other arithmetic  45.9 us (14%)
  waiting for transfers between devices  42.9 us (13%)
  matrix products  32.4 us (10%)
  starting transfers between devices  31.4 us (10%)
  between operations  18.9 us (6%)
    pallas_call x1, Pallas kernels, response_attention(): pl.pallas_call(kernel, grid_spec=grid_spec, out_shape=jax.ShapeDtypeStruc...  65.7 us
    all_gather x1, waiting for transfers between devices, body(): finals = lax.all_gather(jnp.stack(chain_finals), 'seq', axis=1, tiled=True)  25.2 us
    another operation x4, local copies, waits for them, and re-layouts, chunked_pass(): xs = inputs.reshape(blocks, QS, heads, SP).transpose(0, 2, 1, 3)  21.2 us
    unnamed x40, other arithmetic  21.1 us
    dot_general x4, matrix products, chunked_pass(): jnp.einsum('ctn,chpn->chtp', cs.astype(jnp.float32), before, precision=la...  11.6 us
    all_to_all x1, waiting for transfers between devices, body(): lax.all_to_all(prompt_x, 'seq', split_axis=2, concat_axis=1, tiled=True)  11 us
    unnamed x90, local copies, waits for them, and re-layouts  10.8 us
    dot_general x2, matrix products, body(): jnp.einsum('tn,hdn->thd', resp_c[item].astype(jnp.float32), initial, prec...  9.27 us
  transfers between devices with their start and end apart: 9, of which 3 were waited for; matrix products, arithmetic and copies ran while one was open for 43% of the time, Pallas kernels for 20%

profile of v4, /device:TPU:65, one launch (start us, length us, event | category | flops | bytes accessed | tf_op | source)
XLA Modules:
  0.0 321.6 jit_solution(7682341683934638713)
XLA Ops:
  9.3 6.8 %all-to-all-start.2 = ((f32[2,32,128]{2,0,1:T(2,128)}), f32[2,32,128]{2,0,1:T(2,128)}, u32[]{:S(2)}, u32[]{:S(2)}) async-start(f32[2,32,128]{2,0,1:T(2,128)} %copy.107), calls=%async_computation.2 | async-start | bytes 65536 | tf_op jit(solution)/shard_map/all_to_all | solution.py:172
  30.9 4.0 %fusion.70 = (bf16[1,1024,1024]{2,1,0:T(8,128)(2,1)S(1)}, bf16[1,1024,1024]{2,1,0:T(8,128)(2,1)}) fusion(bf16[2,1024,1024]{2,1,0:T(8,128)(2,1)} %param.25), kind=kLoop, calls=%fused_computation.299 | loop fusion | bytes 8388608 | tf_op jit(solution)/shard_map/slice | solution.py:168
  34.9 3.9 %reshape.661 = bf16[8,128,16,64]{3,2,1,0:T(8,128)(2,1)} reshape(bf16[1,1024,1024]{2,1,0:T(8,128)(2,1)S(1)} %get-tuple-element.107) | data formatting | bytes 4194304 | tf_op jit(solution)/shard_map/reshape;squeeze | solution.py:76
  38.8 5.0 %copy.104 = bf16[8,128,16,64]{1,3,2,0:T(8,128)(2,1)S(1)} copy(bf16[8,128,16,64]{3,2,1,0:T(8,128)(2,1)} %reshape.661) | data formatting | bytes 4194304 | tf_op jit(solution)/shard_map/reshape;squeeze | solution.py:76
  49.1 6.3 %reshape.662 = bf16[8,128,16,64]{3,2,1,0:T(8,128)(2,1)} reshape(bf16[1,1024,1024]{2,1,0:T(8,128)(2,1)} %get-tuple-element.108) | data formatting | bytes 4194304 | tf_op jit(solution)/shard_map/reshape;squeeze | solution.py:76
  55.5 5.9 %copy.117 = bf16[8,128,16,64]{1,3,2,0:T(8,128)(2,1)} copy(bf16[8,128,16,64]{3,2,1,0:T(8,128)(2,1)} %reshape.662) | data formatting | bytes 4194304 | tf_op jit(solution)/shard_map/reshape;squeeze | solution.py:76
  68.3 3.0 fusion
  71.4 3.0 fusion.1
  74.7 3.9 %fusion.5 = f32[8,16,8,8,128]{4,3,2,1,0:T(8,128)} fusion(f32[8,16,128,64]{2,3,1,0:T(8,128)S(1)} %fusion, f32[8,16,64,128]{3,2,1,0:T(8,128)S(1)} %fusion.47, bf16[8,128,128,1]{2,1,3,0:T(8,128)(2,1)S(1)} %bitcast.367, f32[8,128,16]{1,2,0:T(8,128)S(1)} %get-tuple-element.125), kind=kOutput, calls=%fused_computation.14 | convolution fusion | flops 1612709888 | bytes 12910592 | tf_op jit(solution)/shard_map/ctn,chpn->chtp/dot_general | solution.py:106
  78.8 3.9 %fusion.3 = f32[8,16,8,8,128]{4,3,2,1,0:T(8,128)} fusion(f32[8,16,128,64]{2,3,1,0:T(8,128)S(1)} %fusion.1, f32[8,16,64,128]{3,2,1,0:T(8,128)S(1)} %fusion.46, bf16[8,128,128,1]{2,1,3,0:T(8,128)(2,1)S(1)} %bitcast.365, f32[8,128,16]{1,2,0:T(8,128)S(1)} %get-tuple-element.127), kind=kOutput, calls=%fused_computation.10 | convolution fusion | flops 1612709888 | bytes 12910592 | tf_op jit(solution)/shard_map/ctn,chpn->chtp/dot_general | solution.py:106
  90.2 4.3 %reshape.641.q_ref = bf16[2,4096,128]{2,1,0:T(8,128)(2,1)} reshape(bf16[2,1024,512]{2,1,0:T(8,128)(2,1)} %param.18) | data formatting | bytes 4194304 | tf_op jit(solution)/shard_map/reshape | solution.py:222
  96.0 6.8 %all-to-all-start.3 = ((bf16[2,128,2048]{1,0,2:T(2,128)(2,1)}), bf16[2,128,2048]{1,0,2:T(2,128)(2,1)S(1)}, u32[]{:S(2)}, u32[]{:S(2)}) async-start(bf16[2,128,2048]{1,0,2:T(2,128)(2,1)} %copy.110), calls=%async_computation.3 | async-start | bytes 2097152 | tf_op jit(solution)/shard_map/all_to_all | solution.py:171
  107.0 11.0 %all-to-all-done.3 = bf16[2,128,2048]{1,0,2:T(2,128)(2,1)S(1)} async-done(((bf16[2,128,2048]{1,0,2:T(2,128)(2,1)}), bf16[2,128,2048]{1,0,2:T(2,128)(2,1)S(1)}, u32[]{:S(2)}, u32[]{:S(2)}) %all-to-all-start.3) | async-done | bytes 1048608 | tf_op jit(solution)/shard_map/all_to_all | solution.py:171
  119.7 4.3 %all-to-all-start.1 = ((bf16[2,128,2048]{1,0,2:T(2,128)(2,1)}), bf16[2,128,2048]{1,0,2:T(2,128)(2,1)}, u32[]{:S(2)}, u32[]{:S(2)}) async-start(bf16[2,128,2048]{1,0,2:T(2,128)(2,1)} %bitcast.7), calls=%async_computation.1 | async-start | bytes 2097152 | tf_op jit(solution)/shard_map/all_to_all | solution.py:162
  146.8 2.8 broadcast_in_dim.58
  149.6 6.6 %all-to-all-start = ((bf16[2,128,2048]{1,0,2:T(2,128)(2,1)}), bf16[2,128,2048]{1,0,2:T(2,128)(2,1)}, u32[]{:S(2)}, u32[]{:S(2)}) async-start(bf16[2,128,2048]{1,0,2:T(2,128)(2,1)} %bitcast.358), calls=%async_computation | async-start | bytes 2097152 | tf_op jit(solution)/shard_map/all_to_all | solution.py:161
  163.1 5.2 %all-to-all-done = bf16[2,128,2048]{1,0,2:T(2,128)(2,1)} async-done(((bf16[2,128,2048]{1,0,2:T(2,128)(2,1)}), bf16[2,128,2048]{1,0,2:T(2,128)(2,1)}, u32[]{:S(2)}, u32[]{:S(2)}) %all-to-all-start) | async-done | bytes 1048608 | tf_op jit(solution)/shard_map/all_to_all | solution.py:161
  187.3 6.7 %all-to-all-start.4 = ((bf16[2,2048,128]{2,0,1:T(2,128)(2,1)}), bf16[2,2048,128]{2,0,1:T(2,128)(2,1)S(1)}, u32[]{:S(2)}, u32[]{:S(2)}) async-start(bf16[2,2048,128]{2,0,1:T(2,128)(2,1)} %copy.131), calls=%async_computation.4 | async-start | bytes 2097152 | tf_op jit(solution)/shard_map/all_to_all | solution.py:186
  194.1 25.2 %all-gather.6.cloned.1.call-done = f32[2,32,64,128]{3,2,1,0:T(8,128)} async-done(((f32[2,2,64,128]{3,2,1,0:T(8,128)}), f32[2,32,64,128]{3,2,1,0:T(8,128)}) %all-gather.6.cloned.1.call-update) | async-done | bytes 2097168 | tf_op jit(solution)/shard_map/all_gather | solution.py:189
  221.8 65.7 %shard_map.175 = bf16[2,4096,128]{2,1,0:T(8,128)(2,1)} custom-call(s32[2]{0:T(128)} %group_ref.1, s32[2]{0:T(128)} %len_ref.1, s32[1]{0:T(128)} %bitcast.head_ref, bf16[2,4096,128]{2,1,0:T(8,128)(2,1)} %reshape.641.q_ref, bf16[2,2048,128]{2,1,0:T(8,128)(2,1)} %bitcast.379, bf16[2,2048,128]{2,1,0:T(8,128)(2,1)} %bitcast.378, bf16[2,1024,1024]{2,1,0:T(8,128)(2,1)} %rk_ref.1, ...), custom_call_target="tpu_custom_call" | custom-call | flops 12884901888 | bytes 7340032 | tf_op jit(solution)/shard_map/pallas_call | solution.py:289
  287.5 4.3 %reshape.644 = bf16[2,1024,512]{2,1,0:T(8,128)(2,1)} reshape(bf16[2,4096,128]{2,1,0:T(8,128)(2,1)} %shard_map.175) | data formatting | bytes 4194304 | tf_op jit(solution)/shard_map/reshape | solution.py:297
  294.0 4.6 %multiply_reduce_fusion.1 = (f32[1024,16]{0,1:T(8,128)S(1)}, f32[1024,16,64]{0,2,1:T(8,128)S(1)}) fusion(bf16[2,1024,128]{2,1,0:T(8,128)(2,1)S(1)} %copy-done.4, f32[2,16,64,128]{3,2,1,0:T(8,128)} %all-reduce.2.cloned.1.call-done, s32[]{:T(128)S(6)} %select_n.79, f32[1024,16]{0,1:T(8,128)S(1)} %bitcast_bitcast_fusion.1, f32[8,16,8,8,128]{4,3,2,1,0:T(8,128)} %fusion.5), kind=kOutput, calls=%fused_computation.23 | convolution fusion | flops 1614790656 | bytes 9306116 | tf_op jit(solution)/shard_map/tn,hdn->thd/dot_general | solution.py:203
  299.3 2.7 copy.114
  302.0 4.6 %multiply_reduce_fusion = (f32[1024,16]{0,1:T(8,128)S(1)}, f32[1024,16,64]{0,2,1:T(8,128)S(1)}) fusion(bf16[2,1024,128]{2,1,0:T(8,128)(2,1)S(1)} %copy-done.4, f32[2,16,64,128]{3,2,1,0:T(8,128)} %all-reduce.2.cloned.1.call-done, s32[]{:T(128)S(6)} %select_n.82, f32[1024,16]{0,1:T(8,128)S(1)} %bitcast_bitcast_fusion, f32[8,16,8,8,128]{4,3,2,1,0:T(8,128)} %fusion.3), kind=kOutput, calls=%fused_computation.16 | convolution fusion | flops 1614790656 | bytes 9306116 | tf_op jit(solution)/shard_map/tn,hdn->thd/dot_general | solution.py:203
  (243 shorter events, 101.7 us)
Async XLA Ops:
  7.2 118.1 %all-gather.4.cloned.1.call-start = ((), (), s32[]{:S(2)}) async-start(), calls=%async_computation.5 | async-start | bytes 1114112 | tf_op jit(solution)/shard_map/all_gather | solution.py:173
  9.3 86.7 %all-to-all-start.2 = ((f32[2,32,128]{2,0,1:T(2,128)}), f32[2,32,128]{2,0,1:T(2,128)}, u32[]{:S(2)}, u32[]{:S(2)}) async-start(f32[2,32,128]{2,0,1:T(2,128)} %copy.107), calls=%async_computation.2 | async-start | bytes 65536 | tf_op jit(solution)/shard_map/all_to_all | solution.py:172
  16.1 154.9 %all-gather.8.cloned.1.call-start = ((), (), s32[]{:S(2)}) async-start(), calls=%async_computation.8 | async-start | bytes 1114112 | tf_op jit(solution)/shard_map/all_gather | solution.py:174
  38.8 5.0 %copy-start.11 = (bf16[2,1024,128]{2,1,0:T(8,128)(2,1)S(1)}, bf16[2,1024,128]{2,1,0:T(8,128)(2,1)}, u32[]{:S(2)}) copy-start(bf16[2,1024,128]{2,1,0:T(8,128)(2,1)} %param.27) | copy-start | bytes 1572868
  78.7 4.1 %copy-start.19 = (f32[16]{0:T(128)S(1)}, f32[16]{0:T(128)}, u32[]{:S(2)}) copy-start(f32[16]{0:T(128)} %get-tuple-element.22) | copy-start | bytes 196
  78.7 4.1 %copy-start.31 = (f32[16]{0:T(128)S(1)}, f32[16]{0:T(128)}, u32[]{:S(2)}) copy-start(f32[16]{0:T(128)} %get-tuple-element.16) | copy-start | bytes 196
  78.7 4.1 %copy-start.32 = (f32[16]{0:T(128)S(1)}, f32[16]{0:T(128)}, u32[]{:S(2)}) copy-start(f32[16]{0:T(128)} %get-tuple-element.17) | copy-start | bytes 196
  78.7 4.1 %copy-start.33 = (f32[16]{0:T(128)S(1)}, f32[16]{0:T(128)}, u32[]{:S(2)}) copy-start(f32[16]{0:T(128)} %get-tuple-element.18) | copy-start | bytes 196
  78.7 4.1 %copy-start.34 = (f32[16]{0:T(128)S(1)}, f32[16]{0:T(128)}, u32[]{:S(2)}) copy-start(f32[16]{0:T(128)} %get-tuple-element.19) | copy-start | bytes 196
  78.7 7.9 %copy-start.39 = (f32[256]{0:T(256)S(1)}, f32[256]{0:T(256)}, u32[]{:S(2)}) copy-start(f32[256]{0:T(256)} %param.29) | copy-start | bytes 3076
  78.8 8.0 %copy-start.10 = (bf16[2,128,2048]{2,1,0:T(8,128)(2,1)S(1)}, bf16[2,128,2048]{2,1,0:T(8,128)(2,1)}, u32[]{:S(2)}) copy-start(bf16[2,128,2048]{2,1,0:T(8,128)(2,1)} %param.21) | copy-start | bytes 3145732
  78.8 10.0 %copy-start.12 = (bf16[2,128,1024]{2,1,0:T(8,128)(2,1)S(1)}, bf16[2,128,1024]{2,1,0:T(8,128)(2,1)}, u32[]{:S(2)}) copy-start(bf16[2,128,1024]{2,1,0:T(8,128)(2,1)} %param.17) | copy-start | bytes 1572868
  78.8 10.4 %copy-start.13 = (bf16[2,128,1024]{2,1,0:T(8,128)(2,1)S(1)}, bf16[2,128,1024]{2,1,0:T(8,128)(2,1)}, u32[]{:S(2)}) copy-start(bf16[2,128,1024]{2,1,0:T(8,128)(2,1)} %param.16) | copy-start | bytes 1572868
  96.0 22.0 %all-to-all-start.3 = ((bf16[2,128,2048]{1,0,2:T(2,128)(2,1)}), bf16[2,128,2048]{1,0,2:T(2,128)(2,1)S(1)}, u32[]{:S(2)}, u32[]{:S(2)}) async-start(bf16[2,128,2048]{1,0,2:T(2,128)(2,1)} %copy.110), calls=%async_computation.3 | async-start | bytes 2097152 | tf_op jit(solution)/shard_map/all_to_all | solution.py:171
  119.7 27.1 %all-to-all-start.1 = ((bf16[2,128,2048]{1,0,2:T(2,128)(2,1)}), bf16[2,128,2048]{1,0,2:T(2,128)(2,1)}, u32[]{:S(2)}, u32[]{:S(2)}) async-start(bf16[2,128,2048]{1,0,2:T(2,128)(2,1)} %bitcast.7), calls=%async_computation.1 | async-start | bytes 2097152 | tf_op jit(solution)/shard_map/all_to_all | solution.py:162
  125.3 10.1 %copy-start.7 = (bf16[1,16,128,128]{2,3,1,0:T(8,128)(2,1)}, bf16[1,16,128,128]{2,3,1,0:T(8,128)(2,1)S(1)}, u32[]{:S(2)}) copy-start(bf16[1,16,128,128]{2,3,1,0:T(8,128)(2,1)S(1)} %get-tuple-element.115) | copy-start | bytes 1572868
  125.3 10.1 %copy-start.5 = (bf16[1,16,128,128]{2,3,1,0:T(8,128)(2,1)S(1)}, bf16[1,16,128,128]{2,3,1,0:T(8,128)(2,1)}, u32[]{:S(2)}) copy-start(bf16[1,16,128,128]{2,3,1,0:T(8,128)(2,1)} %get-tuple-element.116) | copy-start | bytes 1572868
  129.1 17.0 %copy-start.24 = (f32[2]{0:T(128)S(1)}, f32[2]{0:T(128)}, u32[]{:S(2)}) copy-start(f32[2]{0:T(128)} %get-tuple-element.53) | copy-start | bytes 28
  149.6 18.7 %all-to-all-start = ((bf16[2,128,2048]{1,0,2:T(2,128)(2,1)}), bf16[2,128,2048]{1,0,2:T(2,128)(2,1)}, u32[]{:S(2)}, u32[]{:S(2)}) async-start(bf16[2,128,2048]{1,0,2:T(2,128)(2,1)} %bitcast.358), calls=%async_computation | async-start | bytes 2097152 | tf_op jit(solution)/shard_map/all_to_all | solution.py:161
  156.2 63.1 %all-gather.6.cloned.1.call-start = ((), (), s32[]{:S(2)}) async-start(), calls=%async_computation.6 | async-start | bytes 2228224 | tf_op jit(solution)/shard_map/all_gather | solution.py:189
  163.1 9.8 %copy-start.8 = (bf16[1,16,128,128]{2,3,1,0:T(8,128)(2,1)S(1)}, bf16[1,16,128,128]{2,3,1,0:T(8,128)(2,1)}, u32[]{:S(2)}) copy-start(bf16[1,16,128,128]{2,3,1,0:T(8,128)(2,1)} %copy-done.7) | copy-start | bytes 1572868
  173.8 4.8 %copy-start.6 = (bf16[1,16,128,128]{2,3,1,0:T(8,128)(2,1)S(1)}, bf16[1,16,128,128]{2,3,1,0:T(8,128)(2,1)}, u32[]{:S(2)}) copy-start(bf16[1,16,128,128]{2,3,1,0:T(8,128)(2,1)} %get-tuple-element.116) | copy-start | bytes 1572868
  187.3 104.5 %all-to-all-start.4 = ((bf16[2,2048,128]{2,0,1:T(2,128)(2,1)}), bf16[2,2048,128]{2,0,1:T(2,128)(2,1)S(1)}, u32[]{:S(2)}, u32[]{:S(2)}) async-start(bf16[2,2048,128]{2,0,1:T(2,128)(2,1)} %copy.131), calls=%async_computation.4 | async-start | bytes 2097152 | tf_op jit(solution)/shard_map/all_to_all | solution.py:186
  194.1 99.9 %all-reduce.2.cloned.1.call-start = ((), (), s32[]{:S(2)}) async-start(), calls=%async_computation.7 | async-start | bytes 2097152 | tf_op jit(solution)/shard_map/psum | solution.py:27
  (25 other events, 70.2 us)
Sparse Core Ops, SparseCore 0:
  10.2 42.8 all-gather.3
  55.3 41.8 all-gather.7
  159.7 59.5 all-gather.5
  221.9 58.0 all-reduce.1
